TPU v7x, 256 devices: a whole 4x4x8 slice. The times are simulated.
256 devices in a mesh: dp: 64 (over y, z, core), tensor: 4 (over x).
Axes of the slice: x: 4, y: 4, z: 8, core: 2. Of those that a mesh axis runs over, the one named last changes fastest.
Arguments:
- query: bfloat16 [4096, 2560], P('dp', 'tensor'), may hold values from -18 to 18
- new_kv: bfloat16 [2, 4096, 512], P(None, 'dp', 'tensor'), may hold values from -7 to 7
- key_value_pages: bfloat16 [2, 6080, 128, 512], P(None, 'dp', None, 'tensor'), may hold values from -7 to 7
- page_table: int32 [4096, 32], P('dp'), may hold values from 0 to 6079, as said below
- cache_len: int32 [4096], P('dp'), may hold values from 1 to 4096, as said below
- residual: bfloat16 [4096, 2560], P('dp'), may hold values from -6 to 6
- out_weight: bfloat16 [2560, 2560], P('tensor'), may hold values from -0.125 to 0.125
- norm_gain: float32 [2560], replicated, may hold values from 0.25 to 1.75
- expert_ids: int32 [4096, 6], P('dp'), may hold values from 0 to 63, all different within a row; in each aligned block of 64 rows (0 to 63, 64 to 127, ...) at most 9 rows name the same one
- combine_weights: float32 [4096, 6], P('dp'), may hold values from 0.1 to 1
- expert_w1: bfloat16 [64, 2560, 2, 1536], P('dp', None, None, 'tensor'), may hold values from -0.125 to 0.125
- expert_w2: bfloat16 [64, 1536, 2560], P('dp', 'tensor'), may hold values from -0.15625 to 0.15625
Outputs:
- layer_out: bfloat16 [4096, 2560], P('dp', 'tensor')
Inputs may be any that keep to these rules, and one draw needn't show every extreme that they name: `page_table`: entry j of a request's row is the page holding its cache positions j * 128 to (j + 1) * 128 - 1; the pages of request r are among the 95 pages from (r // 64) * 95 on; no page serves two requests; entries past the last used page repeat it. `cache_len`: 6 requests, in 6 different blocks of 64 requests, hold more than (31) * 128 tokens, one of them exactly 4096; all others hold fewer than 64. `expert_ids`: each row names 6 different experts; among the rows of one device (aligned blocks of 64 rows) no expert is named more than 9 times.
All inputs are finite; a program needn't handle non-finite values.
Results may differ from a plain program's by a relative error of at most 0.012.
Values may be sent and summed in bfloat16 or wider, within the bound.
No kernel may reach another device: no remote copies, remote signals or barrier semaphores. Data moves between devices by JAX's collectives and lax.ppermute only.
A program may use at most 128 MiB of HBM per device.

v0:
```python
import math

import jax
import jax.numpy as jnp
from jax import lax
from jax.sharding import PartitionSpec as P

HEAD_SIZE = 128


def local_attention(query, new_kv, key_value_pages, page_table, cache_len):
    row_count = query.shape[0]
    pool_pages = key_value_pages.shape[1]
    page_size = key_value_pages.shape[2]
    head_dim = HEAD_SIZE
    local_heads = new_kv.shape[2] // head_dim
    group_heads = query.shape[1] // (local_heads * head_dim)
    table_width = page_table.shape[1]
    scale_of_score = 1.0 / math.sqrt(head_dim)
    local_pages = page_table - lax.axis_index("dp") * pool_pages
    used_pages = (cache_len + page_size - 1) // page_size
    slot_ids = jnp.arange(table_width, dtype=jnp.int32)
    live_slot = slot_ids[None, :] < used_pages[:, None]
    page_ids = jnp.arange(pool_pages, dtype=jnp.int32)
    onehot = ((local_pages[:, :, None] == page_ids[None, None, :]) & live_slot[:, :, None]).astype(
        jnp.float32
    )
    owner = jnp.sum(onehot, axis=1)
    page_slot = jnp.sum(onehot * slot_ids.astype(jnp.float32)[None, :, None], axis=(0, 1))
    page_len = jnp.dot(cache_len.astype(jnp.float32), owner, precision=lax.Precision.HIGHEST)
    q_pages = jnp.dot(owner.T.astype(jnp.bfloat16), query, preferred_element_type=jnp.float32)
    q_pages = q_pages.astype(jnp.bfloat16).reshape(pool_pages, local_heads, group_heads, head_dim)
    keys_of_page = key_value_pages[0].reshape(pool_pages, page_size, local_heads, head_dim)
    values_of_page = key_value_pages[1].reshape(pool_pages, page_size, local_heads, head_dim)
    scores = (
        jnp.einsum("pkgd,pikd->pkgi", q_pages, keys_of_page, preferred_element_type=jnp.float32)
        * scale_of_score
    )
    position = page_slot[:, None] * page_size + jnp.arange(page_size, dtype=jnp.float32)[None, :]
    valid = position < page_len[:, None]
    scores = jnp.where(valid[:, None, None, :], scores, -1e30)
    page_max = jnp.max(scores, axis=3)
    own_heads = query.reshape(row_count, local_heads, group_heads, head_dim)
    new_keys = new_kv[0].reshape(row_count, local_heads, head_dim)
    new_values = new_kv[1].reshape(row_count, local_heads, head_dim)
    fresh_score = (
        jnp.einsum("rkgd,rkd->rkg", own_heads, new_keys, preferred_element_type=jnp.float32)
        * scale_of_score
    )
    request_max = jnp.max(jnp.where(owner[:, :, None, None] > 0, page_max[None], -1e30), axis=1)
    row_max = jnp.maximum(request_max, fresh_score)
    page_top = jnp.dot(owner.T, row_max.reshape(row_count, -1), precision=lax.Precision.HIGHEST)
    page_top = page_top.reshape(pool_pages, local_heads, group_heads)
    weights = jnp.where(valid[:, None, None, :], jnp.exp(scores - page_top[..., None]), 0.0)
    page_den = jnp.sum(weights, axis=3).reshape(pool_pages, -1)
    page_num = jnp.einsum(
        "pkgi,pikd->pkgd",
        weights.astype(jnp.bfloat16),
        values_of_page,
        preferred_element_type=jnp.float32,
    ).reshape(pool_pages, -1)
    weight_new = jnp.exp(fresh_score - row_max)
    denominator = jnp.dot(owner, page_den, precision=lax.Precision.HIGHEST).reshape(
        row_count, local_heads, group_heads
    )
    denominator = denominator + weight_new
    weighted_numerator = jnp.dot(owner, page_num, precision=lax.Precision.HIGHEST)
    weighted_numerator = weighted_numerator.reshape(row_count, local_heads, group_heads, head_dim)
    weighted_numerator = weighted_numerator + jnp.einsum(
        "rkg,rkd->rkgd",
        weight_new.astype(jnp.bfloat16),
        new_values,
        preferred_element_type=jnp.float32,
    )
    return (weighted_numerator / denominator[..., None]).reshape(row_count, -1).astype(jnp.bfloat16)


def per_device(
    query,
    new_kv,
    key_value_pages,
    page_table,
    cache_len,
    residual,
    out_weight,
    norm_gain,
    expert_ids,
    combine_weights,
    expert_w1,
    expert_w2,
):
    attn = local_attention(query, new_kv, key_value_pages, page_table, cache_len)
    partial_proj = jnp.dot(attn, out_weight, preferred_element_type=jnp.float32)
    row_count, model_width = residual.shape
    share_width = model_width // lax.axis_size("tensor")
    share_start = lax.axis_index("tensor") * share_width
    summed = lax.psum(partial_proj, "tensor")
    state = residual.astype(jnp.float32) + summed
    mean_square = jnp.mean(state * state, axis=1, keepdims=True)
    normed = (state * lax.rsqrt(mean_square + 1e-05) * norm_gain).astype(jnp.bfloat16)
    state_share = lax.dynamic_slice_in_dim(state, share_start, share_width, 1)
    local_experts = expert_w1.shape[0]
    top_count = expert_ids.shape[1]
    experts = local_experts * lax.axis_size("dp")
    capacity = min(
        row_count, max(3, (3 * row_count * top_count + 2 * experts - 1) // (2 * experts))
    )
    flat_ids = expert_ids.reshape(-1)
    choice_rows = flat_ids.shape[0]
    row_iota = jnp.arange(choice_rows, dtype=jnp.int32)
    choice_hot = (flat_ids[:, None] == jnp.arange(experts, dtype=jnp.int32)[None, :]).astype(
        jnp.float32
    )
    strictly_lower = (row_iota[:, None] > row_iota[None, :]).astype(jnp.float32)
    earlier = jnp.dot(strictly_lower, choice_hot, precision=lax.Precision.HIGHEST)
    slot_rank = jnp.sum(earlier * choice_hot, axis=1).astype(jnp.int32)
    slot_index = flat_ids * capacity + slot_rank
    slot_hot = (
        slot_index[:, None] == jnp.arange(experts * capacity, dtype=jnp.int32)[None, :]
    ).astype(jnp.float32)
    token_hot = (
        (row_iota // top_count)[:, None] == jnp.arange(row_count, dtype=jnp.int32)[None, :]
    ).astype(jnp.float32)
    placing = jnp.dot(slot_hot.T, token_hot, precision=lax.Precision.HIGHEST)
    outgoing = jnp.dot(placing.astype(jnp.bfloat16), normed, preferred_element_type=jnp.float32)
    outgoing = outgoing.astype(jnp.bfloat16).reshape(experts, capacity, -1)
    mixing = jnp.dot(
        token_hot.T,
        slot_hot * combine_weights.reshape(-1)[:, None],
        precision=lax.Precision.HIGHEST,
    )
    arrived = lax.all_to_all(outgoing, "dp", split_axis=0, concat_axis=0, tiled=True)
    sources = arrived.shape[0] // local_experts
    item_count = arrived.shape[1]
    arrived_rows = arrived.reshape(sources, local_experts, item_count, model_width)
    gate_up = jnp.einsum(
        "send,edcf->sencf", arrived_rows, expert_w1, preferred_element_type=jnp.float32
    )
    activated = (jax.nn.silu(gate_up[..., 0, :]) * gate_up[..., 1, :]).astype(jnp.bfloat16)
    partial_out = jnp.einsum(
        "senf,efd->send", activated, expert_w2, preferred_element_type=jnp.float32
    )
    partial_out = partial_out.reshape(sources * local_experts, item_count, model_width)
    expert_sum = lax.psum_scatter(
        partial_out.astype(jnp.bfloat16), "tensor", scatter_dimension=2, tiled=True
    )
    returned_rows = lax.all_to_all(expert_sum, "dp", split_axis=0, concat_axis=0, tiled=True)
    expert_mix = jnp.dot(
        mixing,
        returned_rows.reshape(experts * capacity, -1).astype(jnp.float32),
        precision=lax.Precision.HIGHEST,
    )
    return (state_share + expert_mix).astype(jnp.bfloat16)


def solution(mesh):
    return jax.shard_map(
        per_device,
        mesh=mesh,
        in_specs=(
            P("dp", "tensor"),
            P(None, "dp", "tensor"),
            P(None, "dp", None, "tensor"),
            P("dp", None),
            P("dp"),
            P("dp", None),
            P("tensor", None),
            P(),
            P("dp", None),
            P("dp", None),
            P("dp", None, None, "tensor"),
            P("dp", "tensor", None),
        ),
        out_specs=P("dp", "tensor"),
        check_vma=False,
    )
```

profile of v0, /device:TPU:1, one launch (start us, length us, event | category | flops | bytes accessed | tf_op | source)
XLA Modules:
  0.0 362.5 jit_solution(4747731906453002867)
XLA Ops:
  6.5 0.9 broadcast_subtract_fusion
  9.0 0.8 convolution_bitcast_fusion
  10.4 1.7 convolution_convert_fusion.2
  12.2 1.6 reshape.226
  13.8 1.1 reshape.224
  15.0 4.4 %fusion.69 = (f32[95,5]{1,0:T(8,128)S(1)}, f32[95,5,128]{2,1,0:T(8,128)}) fusion(bf16[95,5,128]{2,1,0:T(8,128)(2,1)S(1)} %reshape.224, bf16[2,95,128,128]{3,2,1,0:T(8,128)(2,1)} %param.14, pred[95,128]{1,0:T(8,128)(4,1)S(1)} %add_compare_fusion), kind=kOutput, calls=%fused_computation.101 | convolution fusion | flops 15746725 | bytes 3491820 | tf_op jit(solution)/shard_map/pkgd,pikd->pkgi/dot_general | solution.py:36
  19.4 1.4 bitcast_convert_fusion
  20.8 1.1 fusion.53
  22.0 0.8 select_reduce_fusion.1
  23.1 1.3 fusion.39
  24.4 3.0 fusion.3
  28.0 0.8 convolution_add_fusion.2
  28.9 0.8 dot_general.70
  29.7 1.4 fusion.25
  31.1 1.6 fusion.48
  33.6 49.5 %all-reduce.2.cloned.1.call-done = f32[64,2560]{1,0:T(8,128)} async-done(((f32[64,2560]{1,0:T(8,128)}), f32[64,2560]{1,0:T(8,128)}) %all-reduce.2.cloned.1.call-update) | async-done | bytes 655376 | tf_op jit(solution)/shard_map/psum | solution.py:97
  83.1 1.4 multiply_reduce_fusion
  84.5 0.8 copy-done.1
  85.3 2.5 convolution_convert_fusion.1
  87.9 5.1 %reshape.232 = bf16[64,9,2560]{2,1,0:T(8,128)(2,1)} reshape(bf16[576,2560]{1,0:T(8,128)(2,1)} %convolution_convert_fusion.1) | data formatting | bytes 5898240 | tf_op jit(solution)/shard_map/reshape | solution.py:126
  93.0 131.8 %all_to_all.10 = bf16[64,9,2560]{2,1,0:T(8,128)(2,1)S(1)} all-to-all(bf16[64,9,2560]{2,1,0:T(8,128)(2,1)} %reshape.232), channel_id=1, replica_groups=mesh['dp'=64,'tensor'=4] {'dp'}, dimensions={0} | all-to-all | bytes 5898240 | tf_op jit(solution)/shard_map/all_to_all | solution.py:132
  224.8 5.0 %fusion.11 = f32[64,1,9,2,384]{4,0,3,2,1:T(8,128)S(1)} fusion(bf16[2560,2,384]{2,1,0:T(2,128)(2,1)S(1)} %bitcast.90, bf16[64,9,2560,1]{2,1,0,3:T(8,128)(2,1)S(1)} %bitcast.87), kind=kOutput, calls=%fused_computation.13 | convolution fusion | flops 2264924160 | bytes 8650752 | tf_op jit(solution)/shard_map/send,edcf->sencf/dot_general | solution.py:136
  229.8 3.4 convolution_convert_fusion
  233.2 12.2 %copy.60 = bf16[64,9,2560]{0,1,2:T(8,128)(2,1)} copy(bf16[64,9,2560]{2,0,1:T(8,128)(2,1)} %convolution_convert_fusion) | data formatting | bytes 5898240
  245.3 12.7 %reshape.245 = bf16[2560,576]{1,0:T(8,128)(2,1)} reshape(bf16[2560,9,64]{2,1,0:T(8,128)(2,1)} %bitcast.85) | data formatting | bytes 5898240
  258.1 37.9 %reduce-scatter.4.cloned.1.call-done = bf16[640,576]{1,0:T(8,128)(2,1)} async-done(((bf16[2560,576]{1,0:T(8,128)(2,1)}), bf16[640,576]{1,0:T(8,128)(2,1)}) %reduce-scatter.4.cloned.1.call-update) | async-done | bytes 737296
  295.9 3.9 %reshape.246 = bf16[640,9,64]{2,1,0:T(8,128)(2,1)} reshape(bf16[640,576]{1,0:T(8,128)(2,1)} %reduce-scatter.4.cloned.1.call-done) | data formatting | bytes 1474560
  299.9 6.2 %copy.53 = bf16[64,9,640]{2,1,0:T(8,128)(2,1)} copy(bf16[64,9,640]{0,1,2:T(8,128)(2,1)} %bitcast.86) | data formatting | bytes 1474560 | tf_op jit(solution)/shard_map/reduce_scatter | solution.py:144
  306.1 10.9 %all-to-all-start.1 = ((bf16[64,9,640]{2,1,0:T(8,128)(2,1)}), bf16[64,9,640]{2,1,0:T(8,128)(2,1)}, u32[]{:S(2)}, u32[]{:S(2)}) async-start(bf16[64,9,640]{2,1,0:T(8,128)(2,1)} %copy.53), calls=%async_computation.1 | async-start | bytes 2621440 | tf_op jit(solution)/shard_map/all_to_all | solution.py:147
  318.0 33.1 %all-to-all-done.1 = bf16[64,9,640]{2,1,0:T(8,128)(2,1)} async-done(((bf16[64,9,640]{2,1,0:T(8,128)(2,1)}), bf16[64,9,640]{2,1,0:T(8,128)(2,1)}, u32[]{:S(2)}, u32[]{:S(2)}) %all-to-all-start.1) | async-done | bytes 737312 | tf_op jit(solution)/shard_map/all_to_all | solution.py:147
  351.1 2.3 reshape.235
  353.4 2.3 fusion.24
  (42 shorter events, 5.3 us)
Async XLA Ops:
  6.5 24.5 %copy-start = (bf16[640,2560]{1,0:T(8,128)(2,1)S(1)}, bf16[640,2560]{1,0:T(8,128)(2,1)}, u32[]{:S(2)}) copy-start(bf16[640,2560]{1,0:T(8,128)(2,1)} %param.18) | copy-start | bytes 9830404
  6.5 76.6 %all-reduce.2.cloned.1.call-start = ((), (), s32[]{:S(2)}) async-start(), calls=%async_computation.3 | async-start | bytes 1310720 | tf_op jit(solution)/shard_map/psum | solution.py:97
  15.0 4.4 %copy-start.2 = (pred[95,128]{1,0:T(8,128)(4,1)}, pred[95,128]{1,0:T(8,128)(4,1)S(1)}, u32[]{:S(2)}) copy-start(pred[95,128]{1,0:T(8,128)(4,1)S(1)} %add_compare_fusion) | copy-start | bytes 36484
  29.7 3.0 copy-start.4
  31.0 54.3 %copy-start.3 = (f32[2560]{0:T(1024)S(1)}, f32[2560]{0:T(1024)}, u32[]{:S(2)}) copy-start(f32[2560]{0:T(1024)} %param.19) | copy-start | bytes 30724
  32.6 263.3 %reduce-scatter.4.cloned.1.call-start = ((), (), s32[]{:S(2)}) async-start(), calls=%async_computation.4 | async-start | bytes 4096000
  84.5 0.9 copy-start.1
  93.0 131.8 %copy-start.6 = (bf16[1,2560,2,384]{3,2,1,0:T(2,128)(2,1)S(1)}, bf16[1,2560,2,384]{3,2,1,0:T(2,128)(2,1)}, u32[]{:S(2)}) copy-start(bf16[1,2560,2,384]{3,2,1,0:T(2,128)(2,1)} %param.22) | copy-start | bytes 11796484
  224.8 5.0 %copy-start.7 = (bf16[1,384,2560]{2,1,0:T(8,128)(2,1)S(1)}, bf16[1,384,2560]{2,1,0:T(8,128)(2,1)}, u32[]{:S(2)}) copy-start(bf16[1,384,2560]{2,1,0:T(8,128)(2,1)} %param.23) | copy-start | bytes 5898244
  299.9 17.2 %copy-start.5 = (f32[64,6]{0,1:T(8,128)S(1)}, f32[64,6]{0,1:T(8,128)}, u32[]{:S(2)}) copy-start(f32[64,6]{0,1:T(8,128)} %param.21) | copy-start | bytes 4612
  306.1 45.0 %all-to-all-start.1 = ((bf16[64,9,640]{2,1,0:T(8,128)(2,1)}), bf16[64,9,640]{2,1,0:T(8,128)(2,1)}, u32[]{:S(2)}, u32[]{:S(2)}) async-start(bf16[64,9,640]{2,1,0:T(8,128)(2,1)} %copy.53), calls=%async_computation.1 | async-start | bytes 2621440 | tf_op jit(solution)/shard_map/all_to_all | solution.py:147
Sparse Core Ops, SparseCore 0:
  32.8 50.2 all-reduce.1
  258.2 37.6 reduce-scatter.3
where the time goes:
time: 364 us; the launch traced here: 362 us
  blocking collectives  132 us (36%)
  waiting for transfers between devices  121 us (33%)
  local copies, waits for them, and re-layouts  47.5 us (13%)
  matrix products  29.5 us (8%)
  between operations  13.6 us (4%)
  starting transfers between devices  11 us (3%)
  other arithmetic  8.57 us (2%)
    all_to_all x1, blocking collectives, per_device(): lax.all_to_all(outgoing, 'dp', split_axis=0, concat_axis=0, tiled=True)  132 us
    psum x1, waiting for transfers between devices, per_device(): summed = lax.psum(partial_proj, 'tensor')  49.5 us
    unnamed x3, waiting for transfers between devices  37.9 us
    all_to_all x1, waiting for transfers between devices, per_device(): lax.all_to_all(expert_sum, 'dp', split_axis=0, concat_axis=0, tiled=True)  33.1 us
    unnamed x23, local copies, waits for them, and re-layouts  29.9 us
    all_to_all x1, starting transfers between devices, per_device(): lax.all_to_all(expert_sum, 'dp', split_axis=0, concat_axis=0, tiled=True)  10.9 us
  transfers between devices with their start and end apart: 3, of which 3 were waited for; matrix products, arithmetic and copies ran while one was open for 1% of the time, Pallas kernels for 0%

commit v1 on v0

v1 whole, which is shorter than its diff:
```python
import math

import jax
import jax.numpy as jnp
from jax import lax
from jax.sharding import PartitionSpec as P

HEAD_SIZE = 128
SHORT = 64


def masked_softmax_attend(scores, valid, fresh_score, values, fresh_value):
    scores = jnp.where(valid, scores, -1e30)
    row_max = jnp.maximum(jnp.max(scores, axis=-1), fresh_score)
    weights = jnp.where(valid, jnp.exp(scores - row_max[..., None]), 0.0)
    weight_new = jnp.exp(fresh_score - row_max)
    denominator = jnp.sum(weights, axis=-1) + weight_new
    numerator = jnp.einsum(
        "...ht,...td->...hd",
        weights.astype(jnp.bfloat16),
        values,
        preferred_element_type=jnp.float32,
    )
    numerator = numerator + (
        weight_new.astype(jnp.bfloat16).astype(jnp.float32)[..., None]
        * fresh_value.astype(jnp.float32)[..., None, :]
    )
    return numerator / denominator[..., None]


def local_attention(query, new_kv, key_value_pages, page_table, cache_len):
    row_count = query.shape[0]
    pool_pages = key_value_pages.shape[1]
    page_size = key_value_pages.shape[2]
    head_dim = HEAD_SIZE
    local_heads = new_kv.shape[2] // head_dim
    group_heads = query.shape[1] // (local_heads * head_dim)
    table_width = page_table.shape[1]
    scale_of_score = 1.0 / math.sqrt(head_dim)
    local_pages = jnp.clip(page_table - lax.axis_index("dp") * pool_pages, 0, pool_pages - 1)
    heads = query.reshape(row_count, local_heads * group_heads, head_dim)
    new_keys = new_kv[0].reshape(row_count, local_heads * head_dim)
    new_values = new_kv[1].reshape(row_count, local_heads * head_dim)
    fresh_score = (
        jnp.einsum("rhd,rd->rh", heads, new_keys, preferred_element_type=jnp.float32)
        * scale_of_score
    )
    keys = key_value_pages[0].reshape(pool_pages, page_size, local_heads * head_dim)
    values = key_value_pages[1].reshape(pool_pages, page_size, local_heads * head_dim)

    first = local_pages[:, 0]
    short_keys = keys[:, :SHORT][first]
    short_values = values[:, :SHORT][first]
    short_scores = (
        jnp.einsum("rhd,rtd->rht", heads, short_keys, preferred_element_type=jnp.float32)
        * scale_of_score
    )
    short_valid = (jnp.arange(SHORT, dtype=jnp.int32)[None, :] < cache_len[:, None])[:, None, :]
    short_out = masked_softmax_attend(
        short_scores, short_valid, fresh_score, short_values, new_values
    )

    long_row = jnp.argmax(cache_len)
    long_len = cache_len[long_row]
    long_pages = local_pages[long_row]
    long_keys = keys[long_pages].reshape(table_width * page_size, local_heads * head_dim)
    long_values = values[long_pages].reshape(table_width * page_size, local_heads * head_dim)
    long_heads = heads[long_row]
    long_scores = (
        jnp.einsum("hd,td->ht", long_heads, long_keys, preferred_element_type=jnp.float32)
        * scale_of_score
    )
    long_valid = (jnp.arange(table_width * page_size, dtype=jnp.int32) < long_len)[None, :]
    long_out = masked_softmax_attend(
        long_scores, long_valid, fresh_score[long_row], long_values, new_values[long_row]
    )

    is_long = (jnp.arange(row_count, dtype=jnp.int32) == long_row) & (long_len >= SHORT)
    out = jnp.where(is_long[:, None, None], long_out[None], short_out)
    return out.reshape(row_count, -1).astype(jnp.bfloat16)


def per_device(
    query,
    new_kv,
    key_value_pages,
    page_table,
    cache_len,
    residual,
    out_weight,
    norm_gain,
    expert_ids,
    combine_weights,
    expert_w1,
    expert_w2,
):
    tensor_size = lax.axis_size("tensor")
    tensor_index = lax.axis_index("tensor")
    attn = local_attention(query, new_kv, key_value_pages, page_table, cache_len)
    row_count, model_width = residual.shape
    share_width = model_width // tensor_size
    share_start = tensor_index * share_width

    split_weight = out_weight.reshape(out_weight.shape[0], tensor_size, share_width)
    partial_proj = jnp.einsum(
        "rk,kuc->urc", attn, split_weight, preferred_element_type=jnp.float32
    )
    summed = lax.psum_scatter(partial_proj, "tensor", scatter_dimension=0, tiled=True)[0]
    residual_share = lax.dynamic_slice_in_dim(residual, share_start, share_width, 1)
    state = residual_share.astype(jnp.float32) + summed
    square_sum = lax.psum(jnp.sum(state * state, axis=1, keepdims=True), "tensor")
    mean_square = square_sum / model_width
    gain_share = lax.dynamic_slice_in_dim(norm_gain, share_start, share_width, 0)
    normed = (state * lax.rsqrt(mean_square + 1e-05) * gain_share).astype(jnp.bfloat16)

    local_experts = expert_w1.shape[0]
    top_count = expert_ids.shape[1]
    experts = local_experts * lax.axis_size("dp")
    capacity = min(
        row_count, max(3, (3 * row_count * top_count + 2 * experts - 1) // (2 * experts))
    )
    flat_ids = expert_ids.reshape(-1)
    choice_rows = flat_ids.shape[0]
    row_iota = jnp.arange(choice_rows, dtype=jnp.int32)
    choice_hot = (flat_ids[:, None] == jnp.arange(experts, dtype=jnp.int32)[None, :]).astype(
        jnp.bfloat16
    )
    strictly_lower = (row_iota[:, None] > row_iota[None, :]).astype(jnp.bfloat16)
    earlier = jnp.dot(strictly_lower, choice_hot, preferred_element_type=jnp.float32)
    slot_rank = jnp.sum(earlier * choice_hot.astype(jnp.float32), axis=1).astype(jnp.int32)
    slot_index = (flat_ids * capacity + slot_rank).reshape(row_count, top_count)
    slot_ids = jnp.arange(experts * capacity, dtype=jnp.int32)
    hit = slot_index[:, :, None] == slot_ids[None, None, :]
    placing = jnp.any(hit, axis=1).astype(jnp.bfloat16)
    mixing = jnp.sum(jnp.where(hit, combine_weights[:, :, None], 0.0), axis=1)

    outgoing = jnp.dot(placing.T, normed, preferred_element_type=jnp.float32)
    outgoing = outgoing.astype(jnp.bfloat16).reshape(experts, capacity, share_width)
    arrived = lax.all_to_all(outgoing, "dp", split_axis=0, concat_axis=0, tiled=True)
    gathered = lax.all_gather(arrived, "tensor", axis=0, tiled=False)
    split_w1 = expert_w1.reshape(tensor_size, share_width, 2, expert_w1.shape[-1])
    gate_up = jnp.einsum(
        "usnc,ucgf->sngf", gathered, split_w1, preferred_element_type=jnp.float32
    )
    activated = (jax.nn.silu(gate_up[:, :, 0, :]) * gate_up[:, :, 1, :]).astype(jnp.bfloat16)
    split_w2 = expert_w2[0].reshape(expert_w2.shape[1], tensor_size, share_width)
    partial_out = jnp.einsum(
        "snf,fuc->usnc", activated, split_w2, preferred_element_type=jnp.float32
    ).astype(jnp.bfloat16)
    partial_out = partial_out.reshape(tensor_size, experts * capacity, share_width)
    expert_sum = lax.psum_scatter(partial_out, "tensor", scatter_dimension=0, tiled=True)
    expert_sum = expert_sum.reshape(experts, capacity, share_width)
    returned_rows = lax.all_to_all(expert_sum, "dp", split_axis=0, concat_axis=0, tiled=True)
    expert_mix = jnp.dot(
        mixing,
        returned_rows.reshape(experts * capacity, share_width).astype(jnp.float32),
        precision=lax.Precision.HIGHEST,
    )
    return (state + expert_mix).astype(jnp.bfloat16)


def solution(mesh):
    return jax.shard_map(
        per_device,
        mesh=mesh,
        in_specs=(
            P("dp", "tensor"),
            P(None, "dp", "tensor"),
            P(None, "dp", None, "tensor"),
            P("dp", None),
            P("dp"),
            P("dp", None),
            P("tensor", None),
            P(),
            P("dp", None),
            P("dp", None),
            P("dp", None, None, "tensor"),
            P("dp", "tensor", None),
        ),
        out_specs=P("dp", "tensor"),
        check_vma=False,
    )
```

time: 364 us -> 273 us (0.75)
  blocking collectives: 132 us -> 54.8 us
  local copies, waits for them, and re-layouts: 47.5 us -> 31.6 us
  waiting for transfers between devices: 121 us -> 132 us
  matrix products: 29.5 us -> 20.3 us
    all_to_all x1, blocking collectives: 132 us -> 48.3 us  [per_device(): lax.all_to_all(outgoing, 'dp', split_axis=0, concat_axis=0, tiled=True)]
    reduce_scatter x0 -> x2, waiting for transfers between devices: none -> 64.7 us  [the longest x1 39.6 us: per_device(): lax.psum_scatter(partial_out, 'tensor', scatter_dimension=0, tiled=True)]
    psum x1 -> x0, waiting for transfers between devices: 49.5 us -> none  [per_device(): summed = lax.psum(partial_proj, 'tensor')]
    unnamed x3, waiting for transfers between devices: 37.9 us -> 0.05 us
    all_gather x0 -> x1, waiting for transfers between devices: none -> 33.3 us  [per_device(): gathered = lax.all_gather(arrived, 'tensor', axis=0, tiled=False)]
    unnamed x23, local copies, waits for them, and re-layouts: 29.9 us -> 1.8 us
    gather x0 -> x4, local copies, waits for them, and re-layouts: none -> 10.1 us  [the longest x1 3.57 us: local_attention(): keys[long_pages].reshape(table_width * page_size, local_heads * head_dim)]
    dot_general x16 -> x11, matrix products: 29.5 us -> 20.3 us  [the longest x1 5.59 us: per_device(): jnp.einsum('usnc,ucgf->sngf', gathered, split_w1, preferred_element_type=...]
  transfers between devices with their start and end apart: 3 -> 4, of which waited for: 3 -> 4; matrix products, arithmetic and copies ran while one was open for 1% -> 1% of each run, Pallas kernels for 0% -> 0%
where the time goes in v1:
time: 273 us; the launch traced here: 272 us
  waiting for transfers between devices  132 us (48%)
  blocking collectives  54.8 us (20%)
  local copies, waits for them, and re-layouts  31.6 us (12%)
  matrix products  20.3 us (7%)
  between operations  16.1 us (6%)
  starting transfers between devices  11 us (4%)
  other arithmetic  6.15 us (2%)
    all_to_all x1, blocking collectives, per_device(): lax.all_to_all(outgoing, 'dp', split_axis=0, concat_axis=0, tiled=True)  48.3 us
    reduce_scatter x1, waiting for transfers between devices, per_device(): lax.psum_scatter(partial_out, 'tensor', scatter_dimension=0, tiled=True)  39.6 us
    all_to_all x1, waiting for transfers between devices, per_device(): lax.all_to_all(expert_sum, 'dp', split_axis=0, concat_axis=0, tiled=True)  34 us
    all_gather x1, waiting for transfers between devices, per_device(): gathered = lax.all_gather(arrived, 'tensor', axis=0, tiled=False)  33.3 us
    reduce_scatter x1, waiting for transfers between devices, per_device(): lax.psum_scatter(partial_proj, 'tensor', scatter_dimension=0, tiled=True)[0]  25 us
    all_to_all x1, starting transfers between devices, per_device(): lax.all_to_all(expert_sum, 'dp', split_axis=0, concat_axis=0, tiled=True)  10.7 us
    psum x1, blocking collectives, per_device(): lax.psum(jnp.sum(state * state, axis=1, keepdims=True), 'tensor')  6.52 us
    dot_general x1, matrix products, per_device(): jnp.einsum('usnc,ucgf->sngf', gathered, split_w1, preferred_element_type=...  5.59 us
  transfers between devices with their start and end apart: 4, of which 4 were waited for; matrix products, arithmetic and copies ran while one was open for 1% of the time, Pallas kernels for 0%

profile of v1, /device:TPU:1, one launch (start us, length us, event | category | flops | bytes accessed | tf_op | source)
XLA Modules:
  0.0 272.1 jit_solution(12430237188272823948)
XLA Ops:
  6.5 1.4 iota_reduce_fusion
  9.9 1.2 dynamic_slice.22
  14.2 4.2 %slice_bitcast_fusion.1 = (bf16[95,128,128]{2,1,0:T(8,128)(2,1)S(1)}, bf16[95,128,128]{2,1,0:T(8,128)(2,1)S(1)}) fusion(bf16[2,95,128,128]{3,2,1,0:T(8,128)(2,1)} %param.14), kind=kLoop, calls=%fused_computation.13 | loop fusion | bytes 12451840 | tf_op jit(solution)/shard_map/squeeze | solution.py:48
  18.4 1.7 copy-done
  20.0 1.3 slice.44
  21.3 3.6 %gather_fusion = bf16[32,128,128]{2,1,0:T(8,128)(2,1)} fusion(bf16[95,128,128]{2,1,0:T(8,128)(2,1)} %copy-done, s32[1024]{0:T(1024)S(1)} %pad_clamp_fusion.1), kind=kCustom, calls=%fused_computation | custom fusion | bytes 2097280 | tf_op jit(solution)/shard_map/gather | solution.py:66
  24.9 1.6 gather_fusion.1
  26.6 1.3 slice.46
  28.2 1.8 fusion.64
  30.1 3.2 %gather_fusion.2 = bf16[64,64,128]{2,1,0:T(8,128)(2,1)} fusion(bf16[95,64,128]{2,1,0:T(8,128)(2,1)} %slice.44, s32[1024]{0:T(1024)S(1)} %pad_clamp_fusion), kind=kCustom, calls=%fused_computation.2 | custom fusion | bytes 2097408 | tf_op jit(solution)/shard_map/gather | solution.py:52
  33.3 2.0 fusion.63
  36.5 1.7 gather_fusion.3
  38.5 1.7 fusion.19
  40.3 3.5 %fusion.12 = f32[4,64,640]{2,1,0:T(8,128)} fusion(bf16[64,640,1]{1,0,2:T(8,128)(2,1)S(1)} %reshape.191, bf16[80,4,8,640]{3,2,1,0:T(8,128)(2,1)} %bitcast.104), kind=kOutput, calls=%fused_computation.19 | convolution fusion | flops 209715200 | bytes 4014080 | tf_op jit(solution)/shard_map/rk,kuc->urc/dot_general | solution.py:105
  44.6 0.8 dynamic_slice.27
  45.6 25.0 %reduce-scatter.3.cloned.1.call-done = f32[1,64,640]{2,1,0:T(8,128)} async-done(((f32[4,64,640]{2,1,0:T(8,128)}), f32[1,64,640]{2,1,0:T(8,128)}) %reduce-scatter.3.cloned.1.call-update) | async-done | bytes 163856 | tf_op jit(solution)/shard_map/reduce_scatter | solution.py:108
  70.6 1.0 multiply_reduce_fusion
  71.6 6.5 %psum.7 = f32[64,1]{0,1:T(1,128)S(1)} all-reduce(f32[64,1]{0,1:T(1,128)S(1)} %bitcast.107), channel_id=1, replica_groups=mesh['dp'=64,'tensor'=4] {'tensor'}, use_global_device_ids=true, to_apply=%region_10.11 | all-reduce | flops 64 | bytes 512 | tf_op jit(solution)/shard_map/psum | solution.py:111
  78.2 1.3 convolution_convert_fusion
  79.8 48.3 %all_to_all.10 = bf16[64,9,640]{2,1,0:T(8,128)(2,1)S(1)} all-to-all(bf16[64,9,640]{2,1,0:T(8,128)(2,1)S(1)} %reshape.149), channel_id=1, replica_groups=mesh['dp'=64,'tensor'=4] {'dp'}, dimensions={0} | all-to-all | bytes 1474560 | tf_op jit(solution)/shard_map/all_to_all | solution.py:139
  128.1 1.1 copy.51
  129.4 2.0 reshape_squeeze.3
  131.4 33.3 %all-gather.3.cloned.1.call-done = bf16[256,9,640]{2,0,1:T(8,128)(2,1)} async-done(((bf16[64,9,640]{2,0,1:T(8,128)(2,1)}), bf16[256,9,640]{2,0,1:T(8,128)(2,1)}) %all-gather.3.cloned.1.call-update) | async-done | bytes 2949136 | tf_op jit(solution)/shard_map/all_gather | solution.py:140
  164.8 5.6 %fusion.9 = f32[64,9,2,384]{3,0,2,1:T(8,128)S(1)} fusion(bf16[4,64,9,640,1]{3,1,0,4,2:T(8,128)(2,1)} %bitcast.109, bf16[4,640,2,384]{3,2,1,0:T(2,128)(2,1)} %bitcast.108), kind=kOutput, calls=%fused_computation.17 | convolution fusion | flops 2264924160 | bytes 8650752 | tf_op jit(solution)/shard_map/usnc,ucgf->sngf/dot_general | solution.py:142
  170.4 1.7 convert_bitcast_fusion
  172.1 2.3 copy.54
  174.4 2.0 copy.55
  176.4 39.6 %reduce-scatter.5.cloned.1.call-done = bf16[1,576,640]{2,1,0:T(8,128)(2,1)} async-done(((bf16[4,576,640]{2,1,0:T(8,128)(2,1)}), bf16[1,576,640]{2,1,0:T(8,128)(2,1)}) %reduce-scatter.5.cloned.1.call-update) | async-done | bytes 737296 | tf_op jit(solution)/shard_map/reduce_scatter | solution.py:151
  216.1 2.3 reshape.152
  218.3 10.7 %all-to-all-start.1 = ((bf16[64,9,640]{2,1,0:T(8,128)(2,1)}), bf16[64,9,640]{2,1,0:T(8,128)(2,1)S(1)}, u32[]{:S(2)}, u32[]{:S(2)}) async-start(bf16[64,9,640]{2,1,0:T(8,128)(2,1)} %reshape.152), calls=%async_computation.3 | async-start | bytes 2621440 | tf_op jit(solution)/shard_map/all_to_all | solution.py:153
  229.3 34.0 %all-to-all-done.1 = bf16[64,9,640]{2,1,0:T(8,128)(2,1)S(1)} async-done(((bf16[64,9,640]{2,1,0:T(8,128)(2,1)}), bf16[64,9,640]{2,1,0:T(8,128)(2,1)S(1)}, u32[]{:S(2)}, u32[]{:S(2)}) %all-to-all-start.1) | async-done | bytes 737312 | tf_op jit(solution)/shard_map/all_to_all | solution.py:153
  263.6 2.0 fusion.20
  (60 shorter events, 6.3 us)
Async XLA Ops:
  6.5 64.0 %reduce-scatter.3.cloned.1.call-start = ((), (), s32[]{:S(2)}) async-start(), calls=%async_computation.4 | async-start | bytes 819200 | tf_op jit(solution)/shard_map/reduce_scatter | solution.py:108
  18.4 1.7 copy-start
  24.9 3.0 %copy-start.7 = (bf16[64,640]{1,0:T(8,128)(2,1)S(1)}, bf16[64,640]{1,0:T(8,128)(2,1)}, u32[]{:S(2)}) copy-start(bf16[64,640]{1,0:T(8,128)(2,1)} %param.12) | copy-start | bytes 245764
  24.9 3.1 %copy-start.8 = (bf16[2,64,128]{2,1,0:T(8,128)(2,1)S(1)}, bf16[2,64,128]{2,1,0:T(8,128)(2,1)}, u32[]{:S(2)}) copy-start(bf16[2,64,128]{2,1,0:T(8,128)(2,1)} %param.13) | copy-start | bytes 98308
  28.0 8.5 %copy-start.1 = (bf16[95,64,128]{2,1,0:T(8,128)(2,1)S(1)}, bf16[95,64,128]{2,1,0:T(8,128)(2,1)}, u32[]{:S(2)}) copy-start(bf16[95,64,128]{2,1,0:T(8,128)(2,1)} %slice.46) | copy-start | bytes 4669444
  30.1 8.1 %copy-start.2 = (bf16[32,128,128]{2,1,0:T(8,128)(2,1)S(1)}, bf16[32,128,128]{2,1,0:T(8,128)(2,1)}, u32[]{:S(2)}) copy-start(bf16[32,128,128]{2,1,0:T(8,128)(2,1)} %gather_fusion.1) | copy-start | bytes 3145732
  40.2 3.7 %copy-start.9 = (s32[64,6]{0,1:T(8,128)S(1)}, s32[64,6]{0,1:T(8,128)}, u32[]{:S(2)}) copy-start(s32[64,6]{0,1:T(8,128)} %param.20) | copy-start | bytes 4612
  40.2 30.4 %copy-start.6 = (bf16[64,2560]{1,0:T(8,128)(2,1)S(1)}, bf16[64,2560]{1,0:T(8,128)(2,1)}, u32[]{:S(2)}) copy-start(bf16[64,2560]{1,0:T(8,128)(2,1)} %param.17) | copy-start | bytes 983044
  43.8 121.0 %all-gather.3.cloned.1.call-start = ((), (), s32[]{:S(2)}) async-start(), calls=%async_computation.6 | async-start | bytes 3686400 | tf_op jit(solution)/shard_map/all_gather | solution.py:140
  79.8 49.6 %copy-start.3 = (bf16[1,384,2560]{2,1,0:T(8,128)(2,1)S(1)}, bf16[1,384,2560]{2,1,0:T(8,128)(2,1)}, u32[]{:S(2)}) copy-start(bf16[1,384,2560]{2,1,0:T(8,128)(2,1)} %param.23) | copy-start | bytes 5898244
  129.2 86.9 %reduce-scatter.5.cloned.1.call-start = ((), (), s32[]{:S(2)}) async-start(), calls=%async_computation.5 | async-start | bytes 3686400 | tf_op jit(solution)/shard_map/reduce_scatter | solution.py:151
  164.8 5.6 %copy-start.4 = (bf16[384,4,640]{2,1,0:T(4,128)(2,1)S(1)}, bf16[384,4,640]{2,1,0:T(4,128)(2,1)}, u32[]{:S(2)}) copy-start(bf16[384,4,640]{2,1,0:T(4,128)(2,1)} %reshape_squeeze.3) | copy-start | bytes 5898244
  176.4 52.7 %copy-start.10 = (f32[64,6]{0,1:T(8,128)S(1)}, f32[64,6]{0,1:T(8,128)}, u32[]{:S(2)}) copy-start(f32[64,6]{0,1:T(8,128)} %param.21) | copy-start | bytes 4612
  176.4 87.1 %copy-start.5 = (f32[1,64,640]{2,1,0:T(8,128)S(1)}, f32[1,64,640]{2,1,0:T(8,128)}, u32[]{:S(2)}) copy-start(f32[1,64,640]{2,1,0:T(8,128)} %reduce-scatter.3.cloned.1.call-done) | copy-start | bytes 491524
  218.3 44.9 %all-to-all-start.1 = ((bf16[64,9,640]{2,1,0:T(8,128)(2,1)}), bf16[64,9,640]{2,1,0:T(8,128)(2,1)S(1)}, u32[]{:S(2)}, u32[]{:S(2)}) async-start(bf16[64,9,640]{2,1,0:T(8,128)(2,1)} %reshape.152), calls=%async_computation.3 | async-start | bytes 2621440 | tf_op jit(solution)/shard_map/all_to_all | solution.py:153
Sparse Core Ops, SparseCore 0:
  43.9 26.6 reduce-scatter.2
  129.3 35.4 all-gather.2
  176.5 39.4 reduce-scatter.4

commit v2 on v1

--- a/solution.py
+++ b/solution.py
@@ -3,29 +3,117 @@
 import jax
 import jax.numpy as jnp
 from jax import lax
+from jax.experimental import pallas as pl
+from jax.experimental.pallas import tpu as pltpu
 from jax.sharding import PartitionSpec as P
 
 HEAD_SIZE = 128
 SHORT = 64
 
 
-def masked_softmax_attend(scores, valid, fresh_score, values, fresh_value):
-    scores = jnp.where(valid, scores, -1e30)
-    row_max = jnp.maximum(jnp.max(scores, axis=-1), fresh_score)
-    weights = jnp.where(valid, jnp.exp(scores - row_max[..., None]), 0.0)
-    weight_new = jnp.exp(fresh_score - row_max)
-    denominator = jnp.sum(weights, axis=-1) + weight_new
-    numerator = jnp.einsum(
-        "...ht,...td->...hd",
-        weights.astype(jnp.bfloat16),
-        values,
-        preferred_element_type=jnp.float32,
-    )
-    numerator = numerator + (
-        weight_new.astype(jnp.bfloat16).astype(jnp.float32)[..., None]
-        * fresh_value.astype(jnp.float32)[..., None, :]
-    )
-    return numerator / denominator[..., None]
+def attention_kernel(
+    first_ref, long_ref, info_ref, q_ref, new_k_ref, new_v_ref, len_ref, kv_hbm, o_ref,
+    short_k, short_v, long_k, long_v, sem,
+):
+    rows = q_ref.shape[0]
+    head_dim = new_k_ref.shape[1]
+    groups = q_ref.shape[1] // head_dim
+    table_width = long_ref.shape[0]
+    page_size = kv_hbm.shape[2]
+    chunk = 16
+    scale_of_score = 1.0 / math.sqrt(head_dim)
+
+    def short_copy(r, which, buf):
+        return pltpu.make_async_copy(
+            kv_hbm.at[which, first_ref[r], pl.ds(0, SHORT), :],
+            buf.at[pl.ds(r * SHORT, SHORT), :],
+            sem.at[which, r],
+        )
+
+    def long_copy(j, which, buf):
+        return pltpu.make_async_copy(
+            kv_hbm.at[which, long_ref[j]],
+            buf.at[pl.ds(j * page_size, page_size), :],
+            sem.at[2 + which, j],
+        )
+
+    @pl.loop(0, rows)
+    def _(r):
+        short_copy(r, 0, short_k).start()
+        short_copy(r, 1, short_v).start()
+
+    @pl.loop(0, table_width)
+    def _(j):
+        long_copy(j, 0, long_k).start()
+        long_copy(j, 1, long_v).start()
+
+    @pl.loop(0, rows)
+    def _(r):
+        short_copy(r, 0, short_k).wait()
+        short_copy(r, 1, short_v).wait()
+
+    def attend(qh, keys, values, valid, new_k, new_v):
+        scores = lax.dot_general(
+            qh, keys, (((1,), (1,)), ((), ())), preferred_element_type=jnp.float32
+        ) * scale_of_score
+        fresh = jnp.sum(
+            qh.astype(jnp.float32) * new_k.astype(jnp.float32), axis=1, keepdims=True
+        ) * scale_of_score
+        scores = jnp.where(valid, scores, -1e30)
+        row_max = jnp.maximum(jnp.max(scores, axis=1, keepdims=True), fresh)
+        weights = jnp.where(valid, jnp.exp(scores - row_max), 0.0)
+        weight_new = jnp.exp(fresh - row_max)
+        denominator = jnp.sum(weights, axis=1, keepdims=True) + weight_new
+        numerator = jnp.dot(
+            weights.astype(jnp.bfloat16), values, preferred_element_type=jnp.float32
+        )
+        numerator = numerator + (
+            weight_new.astype(jnp.bfloat16).astype(jnp.float32) * new_v.astype(jnp.float32)
+        )
+        return (numerator / denominator).astype(o_ref.dtype)
+
+    width = chunk * SHORT
+    row = lax.broadcasted_iota(jnp.int32, (chunk, width), 0)
+    col = lax.broadcasted_iota(jnp.int32, (chunk, width), 1)
+    for c in range(rows // chunk):
+        r0 = c * chunk
+        keys = short_k[r0 * SHORT:(r0 + chunk) * SHORT, :]
+        values = short_v[r0 * SHORT:(r0 + chunk) * SHORT, :]
+        lengths = jnp.minimum(len_ref[r0:r0 + chunk, :], SHORT)
+        valid = (col >= row * SHORT) & (col < row * SHORT + lengths)
+        new_k = new_k_ref[r0:r0 + chunk, :]
+        new_v = new_v_ref[r0:r0 + chunk, :]
+        for h in range(groups):
+            qh = q_ref[r0:r0 + chunk, h * head_dim:(h + 1) * head_dim]
+            o_ref[r0:r0 + chunk, h * head_dim:(h + 1) * head_dim] = attend(
+                qh, keys, values, valid, new_k, new_v
+            )
+
+    @pl.loop(0, table_width)
+    def _(j):
+        long_copy(j, 0, long_k).wait()
+        long_copy(j, 1, long_v).wait()
+
+    long_row = info_ref[0]
+    long_len = info_ref[1]
+    long_col = lax.broadcasted_iota(jnp.int32, (chunk, table_width * page_size), 1)
+    long_valid = long_col < long_len
+    own_row = lax.broadcasted_iota(jnp.int32, (chunk, 1), 0)
+    for c in range(rows // chunk):
+        r0 = c * chunk
+
+        @pl.when((long_len >= SHORT) & (long_row >= r0) & (long_row < r0 + chunk))
+        def _():
+            new_k = new_k_ref[r0:r0 + chunk, :]
+            new_v = new_v_ref[r0:r0 + chunk, :]
+            chosen = (own_row + r0) == long_row
+            for h in range(groups):
+                qh = q_ref[r0:r0 + chunk, h * head_dim:(h + 1) * head_dim]
+                result = attend(qh, long_k[...], long_v[...], long_valid, new_k, new_v)
+                current = o_ref[r0:r0 + chunk, h * head_dim:(h + 1) * head_dim]
+                o_ref[r0:r0 + chunk, h * head_dim:(h + 1) * head_dim] = jnp.where(
+                    chosen, result, current
+                )
 
 
 def local_attention(query, new_kv, key_value_pages, page_table, cache_len):
@@ -33,51 +121,42 @@
     pool_pages = key_value_pages.shape[1]
     page_size = key_value_pages.shape[2]
     head_dim = HEAD_SIZE
-    local_heads = new_kv.shape[2] // head_dim
-    group_heads = query.shape[1] // (local_heads * head_dim)
     table_width = page_table.shape[1]
-    scale_of_score = 1.0 / math.sqrt(head_dim)
     local_pages = jnp.clip(page_table - lax.axis_index("dp") * pool_pages, 0, pool_pages - 1)
-    heads = query.reshape(row_count, local_heads * group_heads, head_dim)
-    new_keys = new_kv[0].reshape(row_count, local_heads * head_dim)
-    new_values = new_kv[1].reshape(row_count, local_heads * head_dim)
-    fresh_score = (
-        jnp.einsum("rhd,rd->rh", heads, new_keys, preferred_element_type=jnp.float32)
-        * scale_of_score
-    )
-    keys = key_value_pages[0].reshape(pool_pages, page_size, local_heads * head_dim)
-    values = key_value_pages[1].reshape(pool_pages, page_size, local_heads * head_dim)
-
+    long_row = jnp.argmax(cache_len).astype(jnp.int32)
+    info = jnp.stack([long_row, jnp.max(cache_len)]).astype(jnp.int32)
     first = local_pages[:, 0]
-    short_keys = keys[:, :SHORT][first]
-    short_values = values[:, :SHORT][first]
-    short_scores = (
-        jnp.einsum("rhd,rtd->rht", heads, short_keys, preferred_element_type=jnp.float32)
-        * scale_of_score
-    )
-    short_valid = (jnp.arange(SHORT, dtype=jnp.int32)[None, :] < cache_len[:, None])[:, None, :]
-    short_out = masked_softmax_attend(
-        short_scores, short_valid, fresh_score, short_values, new_values
-    )
-
-    long_row = jnp.argmax(cache_len)
-    long_len = cache_len[long_row]
     long_pages = local_pages[long_row]
-    long_keys = keys[long_pages].reshape(table_width * page_size, local_heads * head_dim)
-    long_values = values[long_pages].reshape(table_width * page_size, local_heads * head_dim)
-    long_heads = heads[long_row]
-    long_scores = (
-        jnp.einsum("hd,td->ht", long_heads, long_keys, preferred_element_type=jnp.float32)
-        * scale_of_score
-    )
-    long_valid = (jnp.arange(table_width * page_size, dtype=jnp.int32) < long_len)[None, :]
-    long_out = masked_softmax_attend(
-        long_scores, long_valid, fresh_score[long_row], long_values, new_values[long_row]
-    )
-
-    is_long = (jnp.arange(row_count, dtype=jnp.int32) == long_row) & (long_len >= SHORT)
-    out = jnp.where(is_long[:, None, None], long_out[None], short_out)
-    return out.reshape(row_count, -1).astype(jnp.bfloat16)
+    smem = pl.BlockSpec(memory_space=pltpu.SMEM)
+    vmem = pl.BlockSpec(memory_space=pltpu.VMEM)
+    rows = row_count * SHORT + table_width * page_size
+    return pl.pallas_call(
+        attention_kernel,
+        out_shape=jax.ShapeDtypeStruct(query.shape, jnp.bfloat16),
+        in_specs=[smem, smem, smem, vmem, vmem, vmem, vmem, pl.BlockSpec(memory_space=pl.ANY)],
+        out_specs=vmem,
+        scratch_shapes=[
+            pltpu.VMEM((row_count * SHORT, head_dim), key_value_pages.dtype),
+            pltpu.VMEM((row_count * SHORT, head_dim), key_value_pages.dtype),
+            pltpu.VMEM((table_width * page_size, head_dim), key_value_pages.dtype),
+            pltpu.VMEM((table_width * page_size, head_dim), key_value_pages.dtype),
+            pltpu.SemaphoreType.DMA((4, row_count)),
+        ],
+        cost_estimate=pl.CostEstimate(
+            flops=4 * 16 * query.shape[1] * rows,
+            transcendentals=16 * query.shape[1] // head_dim * rows,
+            bytes_accessed=2 * 2 * head_dim * rows,
+        ),
+    )(
+        first,
+        long_pages,
+        info,
+        query,
+        new_kv[0],
+        new_kv[1],
+        cache_len[:, None],
+        key_value_pages,
+    )
 
 
 def per_device(

time: 273 us -> 264 us (0.967)
  local copies, waits for them, and re-layouts: 31.6 us -> 15.3 us
  Pallas kernels: 0 us -> 15.1 us
  matrix products: 20.3 us -> 13.4 us
    pallas_call x0 -> x1, Pallas kernels: none -> 15.1 us  [local_attention(): pl.pallas_call(attention_kernel, out_shape=jax.ShapeDtypeStruct(query.sha...]
    gather x4 -> x0, local copies, waits for them, and re-layouts: 10.1 us -> none  [the longest x1 3.57 us: local_attention(): keys[long_pages].reshape(table_width * page_size, local_heads * head_dim)]
    dot_general x5 -> x0, matrix products: 5.99 us -> none  [the longest x2 2 us: masked_softmax_attend(): jnp.einsum('...ht,...td->...hd', weights.astype(jnp.bfloat16), values, pr...]
where the time goes in v2:
time: 264 us; the launch traced here: 263 us
  waiting for transfers between devices  132 us (50%)
  blocking collectives  54.8 us (21%)
  local copies, waits for them, and re-layouts  15.3 us (6%)
  between operations  15.2 us (6%)
  Pallas kernels  15.1 us (6%)
  matrix products  13.4 us (5%)
  starting transfers between devices  11 us (4%)
  other arithmetic  6.74 us (3%)
    all_to_all x1, blocking collectives, per_device(): lax.all_to_all(outgoing, 'dp', split_axis=0, concat_axis=0, tiled=True)  48.3 us
    reduce_scatter x1, waiting for transfers between devices, per_device(): lax.psum_scatter(partial_out, 'tensor', scatter_dimension=0, tiled=True)  39.6 us
    all_to_all x1, waiting for transfers between devices, per_device(): lax.all_to_all(expert_sum, 'dp', split_axis=0, concat_axis=0, tiled=True)  34 us
    all_gather x1, waiting for transfers between devices, per_device(): gathered = lax.all_gather(arrived, 'tensor', axis=0, tiled=False)  33.6 us
    reduce_scatter x1, waiting for transfers between devices, per_device(): lax.psum_scatter(partial_proj, 'tensor', scatter_dimension=0, tiled=True)[0]  24.4 us
    pallas_call x1, Pallas kernels, local_attention(): pl.pallas_call(attention_kernel, out_shape=jax.ShapeDtypeStruct(query.sha...  15.1 us
    all_to_all x1, starting transfers between devices, per_device(): lax.all_to_all(expert_sum, 'dp', split_axis=0, concat_axis=0, tiled=True)  10.8 us
    psum x1, blocking collectives, per_device(): lax.psum(jnp.sum(state * state, axis=1, keepdims=True), 'tensor')  6.52 us
  transfers between devices with their start and end apart: 4, of which 4 were waited for; matrix products, arithmetic and copies ran while one was open for 1% of the time, Pallas kernels for 0%

profile of v2, /device:TPU:1, one launch (start us, length us, event | category | flops | bytes accessed | tf_op | source)
XLA Modules:
  0.0 263.1 jit_solution(16310264230233417726)
XLA Ops:
  6.5 1.3 iota_reduce_fusion
  9.1 0.7 subtract_clamp_fusion
  9.8 0.5 slice_bitcast_fusion.2.first_ref
  11.0 0.7 dynamic-slice_reduce_fusion.long_ref
  11.7 1.3 reduce_max.9
  13.0 1.3 slice_bitcast_fusion
  14.3 1.3 copy.52.len_ref
  15.7 1.9 pad_add_fusion.info_ref
  17.6 15.1 %shard_map.118 = bf16[64,640]{1,0:T(8,128)(2,1)} custom-call(s32[64]{0:T(128)} %slice_bitcast_fusion.2.first_ref, s32[32]{0:T(128)} %dynamic-slice_reduce_fusion.long_ref, s32[2]{0:T(128)} %pad_add_fusion.info_ref, bf16[64,640]{1,0:T(8,128)(2,1)} %q_ref.1, bf16[64,128]{1,0:T(8,128)(2,1)} %get-tuple-element.8.new_k_ref, ...), custom_call_target="tpu_custom_call" | custom-call | flops 335544320 | bytes 4194304 | tf_op jit(solution)/shard_map/pallas_call | solution.py:133
  32.7 2.4 fusion.11
  35.1 0.2 all-gather.3.cloned.1.call-start
  35.6 0.2 fusion.15
  36.1 0.8 dynamic_slice.11
  37.1 24.4 %reduce-scatter.3.cloned.1.call-done = f32[1,64,640]{2,1,0:T(8,128)} async-done(((f32[4,64,640]{2,1,0:T(8,128)}), f32[1,64,640]{2,1,0:T(8,128)}) %reduce-scatter.3.cloned.1.call-update) | async-done | bytes 163856 | tf_op jit(solution)/shard_map/reduce_scatter | solution.py:187
  61.5 1.1 multiply_reduce_fusion
  62.6 6.5 %psum.7 = f32[64,1]{0,1:T(1,128)S(1)} all-reduce(f32[64,1]{0,1:T(1,128)S(1)} %bitcast.65), channel_id=1, replica_groups=mesh['dp'=64,'tensor'=4] {'tensor'}, use_global_device_ids=true, to_apply=%region_7.8 | all-reduce | flops 64 | bytes 512 | tf_op jit(solution)/shard_map/psum | solution.py:190
  69.1 1.4 convolution_convert_fusion
  70.5 0.3 reshape.32
  70.8 48.3 %all_to_all.10 = bf16[64,9,640]{2,1,0:T(8,128)(2,1)S(1)} all-to-all(bf16[64,9,640]{2,1,0:T(8,128)(2,1)S(1)} %reshape.32), channel_id=1, replica_groups=mesh['dp'=64,'tensor'=4] {'dp'}, dimensions={0} | all-to-all | bytes 1474560 | tf_op jit(solution)/shard_map/all_to_all | solution.py:218
  119.1 1.1 copy.56
  120.2 2.0 reshape_squeeze.3
  122.2 33.6 %all-gather.3.cloned.1.call-done = bf16[256,9,640]{2,0,1:T(8,128)(2,1)} async-done(((bf16[64,9,640]{2,0,1:T(8,128)(2,1)}), bf16[256,9,640]{2,0,1:T(8,128)(2,1)}) %all-gather.3.cloned.1.call-update) | async-done | bytes 2949136 | tf_op jit(solution)/shard_map/all_gather | solution.py:219
  155.8 5.6 %fusion.8 = f32[64,9,2,384]{3,0,2,1:T(8,128)S(1)} fusion(bf16[4,64,9,640,1]{3,1,0,4,2:T(8,128)(2,1)} %bitcast.67, bf16[4,640,2,384]{3,2,1,0:T(2,128)(2,1)} %bitcast.66), kind=kOutput, calls=%fused_computation.9 | convolution fusion | flops 2264924160 | bytes 8650752 | tf_op jit(solution)/shard_map/usnc,ucgf->sngf/dot_general | solution.py:221
  161.4 1.7 convert_bitcast_fusion
  163.2 2.3 copy.59
  165.4 2.0 copy.60
  167.4 39.6 %reduce-scatter.5.cloned.1.call-done = bf16[1,576,640]{2,1,0:T(8,128)(2,1)} async-done(((bf16[4,576,640]{2,1,0:T(8,128)(2,1)}), bf16[1,576,640]{2,1,0:T(8,128)(2,1)}) %reduce-scatter.5.cloned.1.call-update) | async-done | bytes 737296 | tf_op jit(solution)/shard_map/reduce_scatter | solution.py:230
  207.1 2.3 reshape.35
  209.3 10.8 %all-to-all-start.1 = ((bf16[64,9,640]{2,1,0:T(8,128)(2,1)}), bf16[64,9,640]{2,1,0:T(8,128)(2,1)S(1)}, u32[]{:S(2)}, u32[]{:S(2)}) async-start(bf16[64,9,640]{2,1,0:T(8,128)(2,1)} %reshape.35), calls=%async_computation.3 | async-start | bytes 2621440 | tf_op jit(solution)/shard_map/all_to_all | solution.py:232
  220.3 34.0 %all-to-all-done.1 = bf16[64,9,640]{2,1,0:T(8,128)(2,1)S(1)} async-done(((bf16[64,9,640]{2,1,0:T(8,128)(2,1)}), bf16[64,9,640]{2,1,0:T(8,128)(2,1)S(1)}, u32[]{:S(2)}, u32[]{:S(2)}) %all-to-all-start.1) | async-done | bytes 737312 | tf_op jit(solution)/shard_map/all_to_all | solution.py:232
  254.3 0.3 reshape.36
  254.6 2.0 fusion.14
  (26 shorter events, 1.0 us)
Async XLA Ops:
  6.5 54.9 %reduce-scatter.3.cloned.1.call-start = ((), (), s32[]{:S(2)}) async-start(), calls=%async_computation.4 | async-start | bytes 819200 | tf_op jit(solution)/shard_map/reduce_scatter | solution.py:187
  17.6 15.1 %copy-start = (bf16[640,2560]{1,0:T(8,128)(2,1)S(1)}, bf16[640,2560]{1,0:T(8,128)(2,1)}, u32[]{:S(2)}) copy-start(bf16[640,2560]{1,0:T(8,128)(2,1)} %param.18) | copy-start | bytes 9830404
  32.7 2.7 %copy-start.4 = (s32[64,6]{0,1:T(8,128)S(1)}, s32[64,6]{0,1:T(8,128)}, u32[]{:S(2)}) copy-start(s32[64,6]{0,1:T(8,128)} %param.20) | copy-start | bytes 4612
  35.1 120.7 %all-gather.3.cloned.1.call-start = ((), (), s32[]{:S(2)}) async-start(), calls=%async_computation.6 | async-start | bytes 3686400 | tf_op jit(solution)/shard_map/all_gather | solution.py:219
  70.8 49.4 %copy-start.1 = (bf16[1,384,2560]{2,1,0:T(8,128)(2,1)S(1)}, bf16[1,384,2560]{2,1,0:T(8,128)(2,1)}, u32[]{:S(2)}) copy-start(bf16[1,384,2560]{2,1,0:T(8,128)(2,1)} %param.23) | copy-start | bytes 5898244
  120.2 86.9 %reduce-scatter.5.cloned.1.call-start = ((), (), s32[]{:S(2)}) async-start(), calls=%async_computation.5 | async-start | bytes 3686400 | tf_op jit(solution)/shard_map/reduce_scatter | solution.py:230
  155.8 5.6 %copy-start.2 = (bf16[384,4,640]{2,1,0:T(4,128)(2,1)S(1)}, bf16[384,4,640]{2,1,0:T(4,128)(2,1)}, u32[]{:S(2)}) copy-start(bf16[384,4,640]{2,1,0:T(4,128)(2,1)} %reshape_squeeze.3) | copy-start | bytes 5898244
  167.4 52.7 %copy-start.5 = (f32[64,6]{0,1:T(8,128)S(1)}, f32[64,6]{0,1:T(8,128)}, u32[]{:S(2)}) copy-start(f32[64,6]{0,1:T(8,128)} %param.21) | copy-start | bytes 4612
  167.4 87.1 %copy-start.3 = (f32[1,64,640]{2,1,0:T(8,128)S(1)}, f32[1,64,640]{2,1,0:T(8,128)}, u32[]{:S(2)}) copy-start(f32[1,64,640]{2,1,0:T(8,128)} %reduce-scatter.3.cloned.1.call-done) | copy-start | bytes 491524
  209.3 44.9 %all-to-all-start.1 = ((bf16[64,9,640]{2,1,0:T(8,128)(2,1)}), bf16[64,9,640]{2,1,0:T(8,128)(2,1)S(1)}, u32[]{:S(2)}, u32[]{:S(2)}) async-start(bf16[64,9,640]{2,1,0:T(8,128)(2,1)} %reshape.35), calls=%async_computation.3 | async-start | bytes 2621440 | tf_op jit(solution)/shard_map/all_to_all | solution.py:232
Sparse Core Ops, SparseCore 0:
  35.3 26.1 reduce-scatter.2
  120.3 35.4 all-gather.2
  167.5 39.4 reduce-scatter.4

commit v3 on v2

--- a/solution.py
+++ b/solution.py
@@ -215,26 +215,39 @@
 
     outgoing = jnp.dot(placing.T, normed, preferred_element_type=jnp.float32)
     outgoing = outgoing.astype(jnp.bfloat16).reshape(experts, capacity, share_width)
-    arrived = lax.all_to_all(outgoing, "dp", split_axis=0, concat_axis=0, tiled=True)
-    gathered = lax.all_gather(arrived, "tensor", axis=0, tiled=False)
+    mixing = mixing.reshape(row_count, experts, capacity)
     split_w1 = expert_w1.reshape(tensor_size, share_width, 2, expert_w1.shape[-1])
-    gate_up = jnp.einsum(
-        "usnc,ucgf->sngf", gathered, split_w1, preferred_element_type=jnp.float32
-    )
-    activated = (jax.nn.silu(gate_up[:, :, 0, :]) * gate_up[:, :, 1, :]).astype(jnp.bfloat16)
     split_w2 = expert_w2[0].reshape(expert_w2.shape[1], tensor_size, share_width)
-    partial_out = jnp.einsum(
-        "snf,fuc->usnc", activated, split_w2, preferred_element_type=jnp.float32
-    ).astype(jnp.bfloat16)
-    partial_out = partial_out.reshape(tensor_size, experts * capacity, share_width)
-    expert_sum = lax.psum_scatter(partial_out, "tensor", scatter_dimension=0, tiled=True)
-    expert_sum = expert_sum.reshape(experts, capacity, share_width)
-    returned_rows = lax.all_to_all(expert_sum, "dp", split_axis=0, concat_axis=0, tiled=True)
-    expert_mix = jnp.dot(
-        mixing,
-        returned_rows.reshape(experts * capacity, share_width).astype(jnp.float32),
-        precision=lax.Precision.HIGHEST,
-    )
+
+    expert_mix = None
+    bounds = [0, (capacity + 1) // 2, capacity]
+    for lo, hi in zip(bounds[:-1], bounds[1:]):
+        slots = hi - lo
+        arrived = lax.all_to_all(
+            outgoing[:, lo:hi], "dp", split_axis=0, concat_axis=0, tiled=True
+        )
+        gathered = lax.all_gather(arrived, "tensor", axis=0, tiled=False)
+        gate_up = jnp.einsum(
+            "usnc,ucgf->sngf", gathered, split_w1, preferred_element_type=jnp.float32
+        )
+        activated = (jax.nn.silu(gate_up[:, :, 0, :]) * gate_up[:, :, 1, :]).astype(
+            jnp.bfloat16
+        )
+        partial_out = jnp.einsum(
+            "snf,fuc->usnc", activated, split_w2, preferred_element_type=jnp.float32
+        ).astype(jnp.bfloat16)
+        partial_out = partial_out.reshape(tensor_size, experts * slots, share_width)
+        expert_sum = lax.psum_scatter(partial_out, "tensor", scatter_dimension=0, tiled=True)
+        expert_sum = expert_sum.reshape(experts, slots, share_width)
+        returned_rows = lax.all_to_all(
+            expert_sum, "dp", split_axis=0, concat_axis=0, tiled=True
+        )
+        part_mix = jnp.dot(
+            mixing[:, :, lo:hi].reshape(row_count, experts * slots),
+            returned_rows.reshape(experts * slots, share_width).astype(jnp.float32),
+            precision=lax.Precision.HIGHEST,
+        )
+        expert_mix = part_mix if expert_mix is None else expert_mix + part_mix
     return (state + expert_mix).astype(jnp.bfloat16)
 
 

time: 264 us -> 255 us (0.966)
  waiting for transfers between devices: 132 us -> 105 us
  starting transfers between devices: 11 us -> 20.8 us
  blocking collectives: 54.8 us -> 60.3 us
  local copies, waits for them, and re-layouts: 15.3 us -> 18.9 us
  Pallas kernels: 15.1 us -> 11.8 us
    all_to_all x1 -> x2, waiting for transfers between devices: 34 us -> 15.8 us  [per_device(): lax.all_to_all(expert_sum, 'dp', split_axis=0, concat_axis=0, tiled=True)]
    all_gather x1 -> x2, waiting for transfers between devices: 33.6 us -> 23.2 us  [per_device(): gathered = lax.all_gather(arrived, 'tensor', axis=0, tiled=False)]
    all_to_all x1 -> x2, starting transfers between devices: 10.8 us -> 20.4 us  [per_device(): lax.all_to_all(expert_sum, 'dp', split_axis=0, concat_axis=0, tiled=True)]
    all_to_all x1 -> x2, blocking collectives: 48.3 us -> 53.7 us  [per_device(): lax.all_to_all(outgoing[:, lo:hi], 'dp', split_axis=0, concat_axis=0, til...]
    pallas_call x1, Pallas kernels: 15.1 us -> 11.8 us  [local_attention(): pl.pallas_call(attention_kernel, out_shape=jax.ShapeDtypeStruct(query.sha...]
    dot_general x1 -> x2, matrix products: 5.59 us -> 7.47 us  [per_device(): jnp.einsum('usnc,ucgf->sngf', gathered, split_w1, preferred_element_type=...]
    reshape x3 -> x5, local copies, waits for them, and re-layouts: 4.56 us -> 6.43 us  [the longest x2 3.77 us: per_device(): expert_sum = expert_sum.reshape(experts, slots, share_width)]
    reduce_scatter x1 -> x2, waiting for transfers between devices: 39.6 us -> 39.2 us  [per_device(): lax.psum_scatter(partial_out, 'tensor', scatter_dimension=0, tiled=True)]
  transfers between devices with their start and end apart: 4 -> 7, of which waited for: 4 -> 7; matrix products, arithmetic and copies ran while one was open for 1% -> 10% of each run, Pallas kernels for 0% -> 0%
where the time goes in v3:
time: 255 us; the launch traced here: 254 us
  waiting for transfers between devices  105 us (41%)
  blocking collectives  60.3 us (24%)
  starting transfers between devices  20.8 us (8%)
  local copies, waits for them, and re-layouts  18.9 us (7%)
  matrix products  15.7 us (6%)
  between operations  15.3 us (6%)
  Pallas kernels  11.8 us (5%)
  other arithmetic  6.74 us (3%)
    all_to_all x2, blocking collectives, per_device(): lax.all_to_all(outgoing[:, lo:hi], 'dp', split_axis=0, concat_axis=0, til...  53.7 us
    reduce_scatter x2, waiting for transfers between devices, per_device(): lax.psum_scatter(partial_out, 'tensor', scatter_dimension=0, tiled=True)  39.2 us
    reduce_scatter x1, waiting for transfers between devices, per_device(): lax.psum_scatter(partial_proj, 'tensor', scatter_dimension=0, tiled=True)[0]  26.4 us
    all_gather x2, waiting for transfers between devices, per_device(): gathered = lax.all_gather(arrived, 'tensor', axis=0, tiled=False)  23.2 us
    all_to_all x2, starting transfers between devices, per_device(): lax.all_to_all(expert_sum, 'dp', split_axis=0, concat_axis=0, tiled=True)  20.4 us
    all_to_all x2, waiting for transfers between devices, per_device(): lax.all_to_all(expert_sum, 'dp', split_axis=0, concat_axis=0, tiled=True)  15.8 us
    pallas_call x1, Pallas kernels, local_attention(): pl.pallas_call(attention_kernel, out_shape=jax.ShapeDtypeStruct(query.sha...  11.8 us
    dot_general x2, matrix products, per_device(): jnp.einsum('usnc,ucgf->sngf', gathered, split_w1, preferred_element_type=...  7.47 us
  transfers between devices with their start and end apart: 7, of which 7 were waited for; matrix products, arithmetic and copies ran while one was open for 10% of the time, Pallas kernels for 0%

profile of v3, /device:TPU:1, one launch (start us, length us, event | category | flops | bytes accessed | tf_op | source)
XLA Modules:
  0.0 254.2 jit_solution(11397129960974430967)
XLA Ops:
  6.5 1.3 iota_reduce_fusion
  7.9 1.3 reduce_max.9
  13.0 1.3 copy.82.len_ref
  14.3 1.3 slice_bitcast_fusion
  15.7 1.9 pad_add_fusion.info_ref
  17.6 11.8 %shard_map.118 = bf16[64,640]{1,0:T(8,128)(2,1)} custom-call(s32[64]{0:T(128)} %slice_bitcast_fusion.2.first_ref, s32[32]{0:T(128)} %dynamic-slice_reduce_fusion.long_ref, s32[2]{0:T(128)} %pad_add_fusion.info_ref, bf16[64,640]{1,0:T(8,128)(2,1)} %q_ref.1, bf16[64,128]{1,0:T(8,128)(2,1)} %get-tuple-element.8.new_k_ref, ...), custom_call_target="tpu_custom_call" | custom-call | flops 335544320 | bytes 4194304 | tf_op jit(solution)/shard_map/pallas_call | solution.py:133
  29.5 2.4 fusion.33
  33.8 26.4 %reduce-scatter.4.cloned.1.call-done = f32[1,64,640]{2,1,0:T(8,128)} async-done(((f32[4,64,640]{2,1,0:T(8,128)}), f32[1,64,640]{2,1,0:T(8,128)}) %reduce-scatter.4.cloned.1.call-update) | async-done | bytes 163856 | tf_op jit(solution)/shard_map/reduce_scatter | solution.py:187
  60.3 1.1 multiply_reduce_fusion
  61.4 6.6 %psum.7 = f32[64,1]{0,1:T(1,128)S(1)} all-reduce(f32[64,1]{0,1:T(1,128)S(1)} %bitcast.111), channel_id=1, replica_groups=mesh['dp'=64,'tensor'=4] {'tensor'}, use_global_device_ids=true, to_apply=%region_7.8 | all-reduce | flops 64 | bytes 512 | tf_op jit(solution)/shard_map/psum | solution.py:190
  68.0 1.4 convolution_convert_fusion
  69.7 34.3 %all_to_all.20 = bf16[64,5,640]{2,1,0:T(8,128)(2,1)S(1)} all-to-all(bf16[64,5,640]{2,1,0:T(8,128)(2,1)S(1)} %slice.46), channel_id=1, replica_groups=mesh['dp'=64,'tensor'=4] {'dp'}, dimensions={0} | all-to-all | bytes 819200 | tf_op jit(solution)/shard_map/all_to_all | solution.py:226
  105.1 19.4 %all_to_all.21 = bf16[64,4,640]{2,1,0:T(4,128)(2,1)} all-to-all(bf16[64,4,640]{2,1,0:T(4,128)(2,1)S(1)} %slice.50), channel_id=1, replica_groups=mesh['dp'=64,'tensor'=4] {'dp'}, dimensions={0} | all-to-all | bytes 655360 | tf_op jit(solution)/shard_map/all_to_all | solution.py:226
  124.6 2.0 reshape_squeeze.3
  126.7 3.0 %all-gather.5.cloned.1.call-done = bf16[256,5,640]{2,0,1:T(8,128)(2,1)} async-done(((bf16[64,5,640]{2,0,1:T(8,128)(2,1)}), bf16[256,5,640]{2,0,1:T(8,128)(2,1)}) %all-gather.5.cloned.1.call-update) | async-done | bytes 1638416 | tf_op jit(solution)/shard_map/all_gather | solution.py:229
  129.7 4.2 %fusion.27 = f32[64,5,2,384]{3,0,2,1:T(8,128)S(1)} fusion(bf16[4,64,5,640,1]{3,1,0,4,2:T(8,128)(2,1)} %bitcast.114, bf16[4,640,2,384]{3,2,1,0:T(2,128)(2,1)} %bitcast.112), kind=kOutput, calls=%fused_computation.20 | convolution fusion | flops 1258291200 | bytes 6553600 | tf_op jit(solution)/shard_map/usnc,ucgf->sngf/dot_general | solution.py:230
  133.9 1.0 fusion.21
  134.9 1.3 copy.91
  136.2 1.4 copy.92
  137.6 20.2 %all-gather.7.cloned.1.call-done = bf16[256,4,640]{2,1,0:T(4,128)(2,1)} async-done(((bf16[64,4,640]{2,1,0:T(4,128)(2,1)}), bf16[256,4,640]{2,1,0:T(4,128)(2,1)}) %all-gather.7.cloned.1.call-update) | async-done | bytes 1310736 | tf_op jit(solution)/shard_map/all_gather | solution.py:229
  157.8 1.5 copy.95
  159.3 3.3 %fusion.30 = f32[64,4,2,384]{3,0,2,1:T(8,128)S(1)} fusion(bf16[4,64,4,640,1]{3,1,0,4,2:T(8,128)(2,1)S(1)} %bitcast.109, bf16[4,640,2,384]{3,2,1,0:T(2,128)(2,1)} %bitcast.113), kind=kOutput, calls=%fused_computation.21 | convolution fusion | flops 1006632960 | bytes 6029312 | tf_op jit(solution)/shard_map/usnc,ucgf->sngf/dot_general | solution.py:230
  164.5 1.2 copy.99
  165.8 24.3 %reduce-scatter.6.cloned.1.call-done = bf16[1,320,640]{2,1,0:T(8,128)(2,1)} async-done(((bf16[4,320,640]{2,1,0:T(8,128)(2,1)}), bf16[1,320,640]{2,1,0:T(8,128)(2,1)}) %reduce-scatter.6.cloned.1.call-update) | async-done | bytes 409616 | tf_op jit(solution)/shard_map/reduce_scatter | solution.py:240
  190.1 2.0 reshape.47
  192.1 11.1 %all-to-all-start.1 = ((bf16[64,5,640]{2,1,0:T(8,128)(2,1)}), bf16[64,5,640]{2,1,0:T(8,128)(2,1)S(1)}, u32[]{:S(2)}, u32[]{:S(2)}) async-start(bf16[64,5,640]{2,1,0:T(8,128)(2,1)} %reshape.47), calls=%async_computation.3 | async-start | bytes 1310720 | tf_op jit(solution)/shard_map/all_to_all | solution.py:242
  203.2 14.9 %reduce-scatter.8.cloned.1.call-done = bf16[1,256,640]{2,1,0:T(8,128)(2,1)} async-done(((bf16[4,256,640]{2,1,0:T(8,128)(2,1)}), bf16[1,256,640]{2,1,0:T(8,128)(2,1)}) %reduce-scatter.8.cloned.1.call-update) | async-done | bytes 327696 | tf_op jit(solution)/shard_map/reduce_scatter | solution.py:240
  218.1 1.8 reshape.49
  219.9 3.4 %all-to-all-done.1 = bf16[64,5,640]{2,1,0:T(8,128)(2,1)S(1)} async-done(((bf16[64,5,640]{2,1,0:T(8,128)(2,1)}), bf16[64,5,640]{2,1,0:T(8,128)(2,1)S(1)}, u32[]{:S(2)}, u32[]{:S(2)}) %all-to-all-start.1) | async-done | bytes 409632 | tf_op jit(solution)/shard_map/all_to_all | solution.py:242
  223.3 9.3 %all-to-all-start.3 = ((bf16[64,4,640]{2,1,0:T(4,128)(2,1)}), bf16[64,4,640]{2,1,0:T(4,128)(2,1)S(1)}, u32[]{:S(2)}, u32[]{:S(2)}) async-start(bf16[64,4,640]{2,1,0:T(4,128)(2,1)} %reshape.49), calls=%async_computation.6 | async-start | bytes 655360 | tf_op jit(solution)/shard_map/all_to_all | solution.py:242
  233.5 12.4 %all-to-all-done.3 = bf16[64,4,640]{2,1,0:T(4,128)(2,1)S(1)} async-done(((bf16[64,4,640]{2,1,0:T(4,128)(2,1)}), bf16[64,4,640]{2,1,0:T(4,128)(2,1)S(1)}, u32[]{:S(2)}, u32[]{:S(2)}) %all-to-all-start.3) | async-done | bytes 327712 | tf_op jit(solution)/shard_map/all_to_all | solution.py:242
  245.9 1.8 fusion.38
  (47 shorter events, 8.2 us)
Async XLA Ops:
  6.5 53.7 %reduce-scatter.4.cloned.1.call-start = ((), (), s32[]{:S(2)}) async-start(), calls=%async_computation.7 | async-start | bytes 819200 | tf_op jit(solution)/shard_map/reduce_scatter | solution.py:187
  17.6 11.9 %copy-start = (bf16[640,2560]{1,0:T(8,128)(2,1)S(1)}, bf16[640,2560]{1,0:T(8,128)(2,1)}, u32[]{:S(2)}) copy-start(bf16[640,2560]{1,0:T(8,128)(2,1)} %param.18) | copy-start | bytes 9830404
  29.5 2.7 %copy-start.4 = (s32[64,6]{0,1:T(8,128)S(1)}, s32[64,6]{0,1:T(8,128)}, u32[]{:S(2)}) copy-start(s32[64,6]{0,1:T(8,128)} %param.20) | copy-start | bytes 4612
  31.9 97.7 %all-gather.5.cloned.1.call-start = ((), (), s32[]{:S(2)}) async-start(), calls=%async_computation.10 | async-start | bytes 2048000 | tf_op jit(solution)/shard_map/all_gather | solution.py:229
  69.7 54.9 %copy-start.1 = (bf16[1,384,2560]{2,1,0:T(8,128)(2,1)S(1)}, bf16[1,384,2560]{2,1,0:T(8,128)(2,1)}, u32[]{:S(2)}) copy-start(bf16[1,384,2560]{2,1,0:T(8,128)(2,1)} %param.23) | copy-start | bytes 5898244
  104.8 53.0 %all-gather.7.cloned.1.call-start = ((), (), s32[]{:S(2)}) async-start(), calls=%async_computation.11 | async-start | bytes 1638400 | tf_op jit(solution)/shard_map/all_gather | solution.py:229
  124.6 65.5 %reduce-scatter.6.cloned.1.call-start = ((), (), s32[]{:S(2)}) async-start(), calls=%async_computation.8 | async-start | bytes 2048000 | tf_op jit(solution)/shard_map/reduce_scatter | solution.py:240
  129.7 4.2 %copy-start.2 = (bf16[384,4,640]{2,1,0:T(4,128)(2,1)S(1)}, bf16[384,4,640]{2,1,0:T(4,128)(2,1)}, u32[]{:S(2)}) copy-start(bf16[384,4,640]{2,1,0:T(4,128)(2,1)} %reshape_squeeze.3) | copy-start | bytes 5898244
  137.6 80.5 %reduce-scatter.8.cloned.1.call-start = ((), (), s32[]{:S(2)}) async-start(), calls=%async_computation.9 | async-start | bytes 1638400 | tf_op jit(solution)/shard_map/reduce_scatter | solution.py:240
  165.8 66.8 %copy-start.5 = (f32[64,6]{0,1:T(8,128)S(1)}, f32[64,6]{0,1:T(8,128)}, u32[]{:S(2)}) copy-start(f32[64,6]{0,1:T(8,128)} %param.21) | copy-start | bytes 4612
  192.1 31.2 %all-to-all-start.1 = ((bf16[64,5,640]{2,1,0:T(8,128)(2,1)}), bf16[64,5,640]{2,1,0:T(8,128)(2,1)S(1)}, u32[]{:S(2)}, u32[]{:S(2)}) async-start(bf16[64,5,640]{2,1,0:T(8,128)(2,1)} %reshape.47), calls=%async_computation.3 | async-start | bytes 1310720 | tf_op jit(solution)/shard_map/all_to_all | solution.py:242
  219.9 26.0 %copy-start.3 = (f32[1,64,640]{2,1,0:T(8,128)S(1)}, f32[1,64,640]{2,1,0:T(8,128)}, u32[]{:S(2)}) copy-start(f32[1,64,640]{2,1,0:T(8,128)} %reduce-scatter.4.cloned.1.call-done) | copy-start | bytes 491524
  223.3 22.6 %all-to-all-start.3 = ((bf16[64,4,640]{2,1,0:T(4,128)(2,1)}), bf16[64,4,640]{2,1,0:T(4,128)(2,1)S(1)}, u32[]{:S(2)}, u32[]{:S(2)}) async-start(bf16[64,4,640]{2,1,0:T(4,128)(2,1)} %reshape.49), calls=%async_computation.6 | async-start | bytes 655360 | tf_op jit(solution)/shard_map/all_to_all | solution.py:242
Sparse Core Ops, SparseCore 0:
  32.0 28.1 reduce-scatter.3
  105.0 24.6 all-gather.4
  131.5 26.3 all-gather.6
  160.3 29.7 reduce-scatter.5
  192.5 25.5 reduce-scatter.7

commit v4 on v3

--- a/solution.py
+++ b/solution.py
@@ -75,17 +75,20 @@
     width = chunk * SHORT
     row = lax.broadcasted_iota(jnp.int32, (chunk, width), 0)
     col = lax.broadcasted_iota(jnp.int32, (chunk, width), 1)
-    for c in range(rows // chunk):
-        r0 = c * chunk
-        keys = short_k[r0 * SHORT:(r0 + chunk) * SHORT, :]
-        values = short_v[r0 * SHORT:(r0 + chunk) * SHORT, :]
-        lengths = jnp.minimum(len_ref[r0:r0 + chunk, :], SHORT)
+
+    @pl.loop(0, rows // chunk)
+    def _(c):
+        r0 = pl.multiple_of(c * chunk, chunk)
+        k0 = pl.multiple_of(c * width, width)
+        keys = short_k[pl.ds(k0, width), :]
+        values = short_v[pl.ds(k0, width), :]
+        lengths = jnp.minimum(len_ref[pl.ds(r0, chunk), :], SHORT)
         valid = (col >= row * SHORT) & (col < row * SHORT + lengths)
-        new_k = new_k_ref[r0:r0 + chunk, :]
-        new_v = new_v_ref[r0:r0 + chunk, :]
+        new_k = new_k_ref[pl.ds(r0, chunk), :]
+        new_v = new_v_ref[pl.ds(r0, chunk), :]
         for h in range(groups):
-            qh = q_ref[r0:r0 + chunk, h * head_dim:(h + 1) * head_dim]
-            o_ref[r0:r0 + chunk, h * head_dim:(h + 1) * head_dim] = attend(
+            qh = q_ref[pl.ds(r0, chunk), h * head_dim:(h + 1) * head_dim]
+            o_ref[pl.ds(r0, chunk), h * head_dim:(h + 1) * head_dim] = attend(
                 qh, keys, values, valid, new_k, new_v
             )
 
@@ -99,21 +102,20 @@
     long_col = lax.broadcasted_iota(jnp.int32, (chunk, table_width * page_size), 1)
     long_valid = long_col < long_len
     own_row = lax.broadcasted_iota(jnp.int32, (chunk, 1), 0)
-    for c in range(rows // chunk):
-        r0 = c * chunk
-
-        @pl.when((long_len >= SHORT) & (long_row >= r0) & (long_row < r0 + chunk))
-        def _():
-            new_k = new_k_ref[r0:r0 + chunk, :]
-            new_v = new_v_ref[r0:r0 + chunk, :]
-            chosen = (own_row + r0) == long_row
-            for h in range(groups):
-                qh = q_ref[r0:r0 + chunk, h * head_dim:(h + 1) * head_dim]
-                result = attend(qh, long_k[...], long_v[...], long_valid, new_k, new_v)
-                current = o_ref[r0:r0 + chunk, h * head_dim:(h + 1) * head_dim]
-                o_ref[r0:r0 + chunk, h * head_dim:(h + 1) * head_dim] = jnp.where(
-                    chosen, result, current
-                )
+
+    @pl.when(long_len >= SHORT)
+    def _():
+        r0 = pl.multiple_of((long_row // chunk) * chunk, chunk)
+        new_k = new_k_ref[pl.ds(r0, chunk), :]
+        new_v = new_v_ref[pl.ds(r0, chunk), :]
+        chosen = (own_row + r0) == long_row
+        for h in range(groups):
+            qh = q_ref[pl.ds(r0, chunk), h * head_dim:(h + 1) * head_dim]
+            result = attend(qh, long_k[...], long_v[...], long_valid, new_k, new_v)
+            current = o_ref[pl.ds(r0, chunk), h * head_dim:(h + 1) * head_dim]
+            o_ref[pl.ds(r0, chunk), h * head_dim:(h + 1) * head_dim] = jnp.where(
+                chosen, result, current
+            )
 
 
 def local_attention(query, new_kv, key_value_pages, page_table, cache_len):
@@ -159,6 +161,22 @@
     )
 
 
+def ring_shift(x, shift, axis_name, size):
+    return lax.ppermute(x, axis_name, [(i, (i + shift) % size) for i in range(size)])
+
+
+def ring_reduce_scatter(blocks, axis_name, size, index):
+    total = lax.dynamic_index_in_dim(blocks, index, 0, keepdims=False).astype(jnp.float32)
+    for shift in range(1, size):
+        outgoing = lax.dynamic_index_in_dim(blocks, (index + shift) % size, 0, keepdims=False)
+        total = total + ring_shift(outgoing, shift, axis_name, size).astype(jnp.float32)
+    return total
+
+
+def ring_all_gather(x, axis_name, size):
+    return [x] + [ring_shift(x, shift, axis_name, size) for shift in range(1, size)]
+
+
 def per_device(
     query,
     new_kv,
@@ -184,10 +202,10 @@
     partial_proj = jnp.einsum(
         "rk,kuc->urc", attn, split_weight, preferred_element_type=jnp.float32
     )
-    summed = lax.psum_scatter(partial_proj, "tensor", scatter_dimension=0, tiled=True)[0]
+    summed = ring_reduce_scatter(partial_proj, "tensor", tensor_size, tensor_index)
     residual_share = lax.dynamic_slice_in_dim(residual, share_start, share_width, 1)
     state = residual_share.astype(jnp.float32) + summed
-    square_sum = lax.psum(jnp.sum(state * state, axis=1, keepdims=True), "tensor")
+    square_sum = sum(ring_all_gather(jnp.sum(state * state, axis=1, keepdims=True), "tensor", tensor_size))
     mean_square = square_sum / model_width
     gain_share = lax.dynamic_slice_in_dim(norm_gain, share_start, share_width, 0)
     normed = (state * lax.rsqrt(mean_square + 1e-05) * gain_share).astype(jnp.bfloat16)
@@ -226,19 +244,22 @@
         arrived = lax.all_to_all(
             outgoing[:, lo:hi], "dp", split_axis=0, concat_axis=0, tiled=True
         )
-        gathered = lax.all_gather(arrived, "tensor", axis=0, tiled=False)
-        gate_up = jnp.einsum(
-            "usnc,ucgf->sngf", gathered, split_w1, preferred_element_type=jnp.float32
-        )
+        pieces = ring_all_gather(arrived, "tensor", tensor_size)
+        gate_up = None
+        for shift, piece in enumerate(pieces):
+            weight = lax.dynamic_index_in_dim(
+                split_w1, (tensor_index - shift) % tensor_size, 0, keepdims=False
+            )
+            term = jnp.einsum("snc,cgf->sngf", piece, weight, preferred_element_type=jnp.float32)
+            gate_up = term if gate_up is None else gate_up + term
         activated = (jax.nn.silu(gate_up[:, :, 0, :]) * gate_up[:, :, 1, :]).astype(
             jnp.bfloat16
         )
         partial_out = jnp.einsum(
             "snf,fuc->usnc", activated, split_w2, preferred_element_type=jnp.float32
         ).astype(jnp.bfloat16)
-        partial_out = partial_out.reshape(tensor_size, experts * slots, share_width)
-        expert_sum = lax.psum_scatter(partial_out, "tensor", scatter_dimension=0, tiled=True)
-        expert_sum = expert_sum.reshape(experts, slots, share_width)
+        expert_sum = ring_reduce_scatter(partial_out, "tensor", tensor_size, tensor_index)
+        expert_sum = expert_sum.astype(jnp.bfloat16)
         returned_rows = lax.all_to_all(
             expert_sum, "dp", split_axis=0, concat_axis=0, tiled=True
         )

time: 255 us -> 210 us (0.82)
  blocking collectives: 60.3 us -> 0 us
  starting transfers between devices: 20.8 us -> 67.8 us
  waiting for transfers between devices: 105 us -> 80.8 us
  between operations: 15.3 us -> 2.35 us
  local copies, waits for them, and re-layouts: 18.9 us -> 22.3 us
    reduce_scatter x3 -> x0, waiting for transfers between devices: 65.6 us -> none  [the longest x2 39.2 us: per_device(): lax.psum_scatter(partial_out, 'tensor', scatter_dimension=0, tiled=True)]
    all_to_all x2 -> x0, blocking collectives: 53.7 us -> none  [per_device(): lax.all_to_all(outgoing[:, lo:hi], 'dp', split_axis=0, concat_axis=0, til...]
    ppermute x0 -> x18, waiting for transfers between devices: none -> 50.2 us  [ring_shift(): lax.ppermute(x, axis_name, [(i, (i + shift) % size) for i in range(size)])]
    ppermute x0 -> x18, starting transfers between devices: none -> 23.2 us  [ring_shift(): lax.ppermute(x, axis_name, [(i, (i + shift) % size) for i in range(size)])]
    all_gather x2 -> x0, waiting for transfers between devices: 23.2 us -> none  [per_device(): gathered = lax.all_gather(arrived, 'tensor', axis=0, tiled=False)]
    all_to_all x0 -> x2, starting transfers between devices: none -> 22.1 us  [per_device(): lax.all_to_all(outgoing[:, lo:hi], 'dp', split_axis=0, concat_axis=0, til...]
    all_to_all x0 -> x2, waiting for transfers between devices: none -> 18.2 us  [per_device(): lax.all_to_all(outgoing[:, lo:hi], 'dp', split_axis=0, concat_axis=0, til...]
    psum x1 -> x0, blocking collectives: 6.58 us -> none  [per_device(): lax.psum(jnp.sum(state * state, axis=1, keepdims=True), 'tensor')]
  transfers between devices with their start and end apart: 7 -> 22, of which waited for: 7 -> 13; matrix products, arithmetic and copies ran while one was open for 10% -> 14% of each run, Pallas kernels for 0% -> 0%
where the time goes in v4:
time: 210 us; the launch traced here: 209 us
  waiting for transfers between devices  80.8 us (38%)
  starting transfers between devices  67.8 us (32%)
  local copies, waits for them, and re-layouts  22.3 us (11%)
  matrix products  17 us (8%)
  Pallas kernels  12.2 us (6%)
  other arithmetic  7.16 us (3%)
  between operations  2.35 us (1%)
    ppermute x18, waiting for transfers between devices, ring_shift(): lax.ppermute(x, axis_name, [(i, (i + shift) % size) for i in range(size)])  50.2 us
    ppermute x18, starting transfers between devices, ring_shift(): lax.ppermute(x, axis_name, [(i, (i + shift) % size) for i in range(size)])  23.2 us
    all_to_all x2, starting transfers between devices, per_device(): lax.all_to_all(expert_sum, 'dp', split_axis=0, concat_axis=0, tiled=True)  22.5 us
    all_to_all x2, starting transfers between devices, per_device(): lax.all_to_all(outgoing[:, lo:hi], 'dp', split_axis=0, concat_axis=0, til...  22.1 us
    all_to_all x2, waiting for transfers between devices, per_device(): lax.all_to_all(outgoing[:, lo:hi], 'dp', split_axis=0, concat_axis=0, til...  18.2 us
    all_to_all x2, waiting for transfers between devices, per_device(): lax.all_to_all(expert_sum, 'dp', split_axis=0, concat_axis=0, tiled=True)  12.4 us
    pallas_call x1, Pallas kernels, local_attention(): pl.pallas_call(attention_kernel, out_shape=jax.ShapeDtypeStruct(query.sha...  12.2 us
    dot_general x8, matrix products, per_device(): jnp.einsum('snc,cgf->sngf', piece, weight, preferred_element_type=jnp.flo...  10.3 us
  transfers between devices with their start and end apart: 22, of which 13 were waited for; matrix products, arithmetic and copies ran while one was open for 14% of the time, Pallas kernels for 0%

profile of v4, /device:TPU:1, one launch (start us, length us, event | category | flops | bytes accessed | tf_op | source)
XLA Modules:
  0.0 209.5 jit_solution(891743156996162269)
XLA Ops:
  9.2 1.9 pad_add_fusion.info_ref
  11.1 12.2 %shard_map.118 = bf16[64,640]{1,0:T(8,128)(2,1)} custom-call(s32[64]{0:T(128)} %slice_bitcast_fusion.2.first_ref, s32[32]{0:T(128)} %dynamic-slice_reduce_fusion.long_ref, s32[2]{0:T(128)} %pad_add_fusion.info_ref, bf16[64,640]{1,0:T(8,128)(2,1)} %q_ref.1, bf16[64,128]{1,0:T(8,128)(2,1)} %get-tuple-element.23.new_k_ref, ...), custom_call_target="tpu_custom_call" | custom-call | flops 335544320 | bytes 4194304 | tf_op jit(solution)/shard_map/pallas_call | solution.py:135
  23.4 1.6 fusion
  25.8 2.1 %collective-permute-start = (f32[64,640]{1,0:T(8,128)S(1)}, f32[64,640]{1,0:T(8,128)S(1)}, u32[]{:S(2)}, u32[]{:S(2)}) collective-permute-start(f32[64,640]{1,0:T(8,128)S(1)} %get-tuple-element.19), channel_id=1, source_target_pairs={{0,1},{1,2},{2,3},{3,0},{4,5},{5,6},{6,7},{7,4},{8,9},{9,10},{10,1... | collective-permute-start | bytes 491528 | tf_op jit(solution)/shard_map/ppermute | solution.py:165
  27.9 2.5 %collective-permute-start.1 = (f32[64,640]{1,0:T(8,128)S(1)}, f32[64,640]{1,0:T(8,128)S(1)}, u32[]{:S(2)}, u32[]{:S(2)}) collective-permute-start(f32[64,640]{1,0:T(8,128)S(1)} %get-tuple-element.21), channel_id=1, source_target_pairs={{0,2},{1,3},{2,0},{3,1},{4,6},{5,7},{6,4},{7,5},{8,10},{9,11},{10,... | collective-permute-start | bytes 491528 | tf_op jit(solution)/shard_map/ppermute | solution.py:165
  32.2 5.3 %collective-permute-done.1 = f32[64,640]{1,0:T(8,128)S(1)} collective-permute-done((f32[64,640]{1,0:T(8,128)S(1)}, f32[64,640]{1,0:T(8,128)S(1)}, u32[]{:S(2)}, u32[]{:S(2)}) %collective-permute-start.1) | collective-permute-done | bytes 163872 | tf_op jit(solution)/shard_map/ppermute | solution.py:165
  39.7 1.9 collective-permute-start.4
  45.7 15.8 %all-to-all-start.2 = ((bf16[64,4,640]{2,1,0:T(4,128)(2,1)}), bf16[64,4,640]{2,1,0:T(4,128)(2,1)S(1)}, u32[]{:S(2)}, u32[]{:S(2)}) async-start(bf16[64,4,640]{2,1,0:T(4,128)(2,1)} %slice.50), calls=%async_computation.2 | async-start | bytes 655360 | tf_op jit(solution)/shard_map/all_to_all | solution.py:244
  62.4 12.4 %all-to-all-done.2 = bf16[64,4,640]{2,1,0:T(4,128)(2,1)S(1)} async-done(((bf16[64,4,640]{2,1,0:T(4,128)(2,1)}), bf16[64,4,640]{2,1,0:T(4,128)(2,1)S(1)}, u32[]{:S(2)}, u32[]{:S(2)}) %all-to-all-start.2) | async-done | bytes 327712 | tf_op jit(solution)/shard_map/all_to_all | solution.py:244
  74.8 6.3 %all-to-all-start = ((bf16[64,5,640]{2,1,0:T(8,128)(2,1)}), bf16[64,5,640]{2,1,0:T(8,128)(2,1)}, u32[]{:S(2)}, u32[]{:S(2)}) async-start(bf16[64,5,640]{2,1,0:T(8,128)(2,1)} %slice.46), calls=%async_computation | async-start | bytes 1310720 | tf_op jit(solution)/shard_map/all_to_all | solution.py:244
  81.2 4.4 %reshape_squeeze.3 = bf16[384,4,640]{2,1,0:T(4,128)(2,1)} reshape(bf16[1,384,2560]{2,1,0:T(8,128)(2,1)} %param.23) | data formatting | bytes 3932160 | tf_op jit(solution)/shard_map/reshape;squeeze | solution.py:238
  85.6 4.2 %constant_dynamic-slice_fusion.1 = (bf16[1,640,2,384]{3,2,1,0:T(2,128)(2,1)S(1)}, bf16[1,640,2,384]{3,2,1,0:T(2,128)(2,1)S(1)}, bf16[1,640,2,384]{3,2,1,0:T(2,128)(2,1)S(1)}, bf16[1,640,2,384]{3,2,1,0:T(2,128)(2,1)S(1)}) fusion(bf16[4,640,2,384]{3,2,1,0:T(2,128)(2,1)} %bitcast.141, s32[]{:T(128)S(6)} %select_n.121, s32[]{:T(128)S(6)} %select_n.119, ...), kind=kLoop, calls=%fused_computation.89 | loop fusion | bytes 7864336 | tf_op jit(solution)/shard_map/jit(dynamic_index_in_dim)/dynamic_slice | solution.py:250
  90.6 2.7 %collective-permute-start.14 = (bf16[64,4,640]{2,0,1:T(8,128)(2,1)}, bf16[64,4,640]{2,0,1:T(8,128)(2,1)}, u32[]{:S(2)}, u32[]{:S(2)}) collective-permute-start(bf16[64,4,640]{2,0,1:T(8,128)(2,1)} %copy.113), channel_id=1, source_target_pairs={{0,3},{1,0},{2,1},{3,2},{4,7},{5,4},{6,5},{7,6},{8,11},{9,8},{10,9... | collective-permute-start | bytes 983048 | tf_op jit(solution)/shard_map/ppermute | solution.py:165
  95.3 5.8 %all-to-all-done = bf16[64,5,640]{2,1,0:T(8,128)(2,1)} async-done(((bf16[64,5,640]{2,1,0:T(8,128)(2,1)}), bf16[64,5,640]{2,1,0:T(8,128)(2,1)}, u32[]{:S(2)}, u32[]{:S(2)}) %all-to-all-start) | async-done | bytes 409632 | tf_op jit(solution)/shard_map/all_to_all | solution.py:244
  102.4 2.7 %collective-permute-start.8 = (bf16[64,5,640]{2,0,1:T(8,128)(2,1)S(1)}, bf16[64,5,640]{2,0,1:T(8,128)(2,1)S(1)}, u32[]{:S(2)}, u32[]{:S(2)}) collective-permute-start(bf16[64,5,640]{2,0,1:T(8,128)(2,1)S(1)} %copy.102), channel_id=1, source_target_pairs={{0,3},{1,0},{2,1},{3,2},{4,7},{5,4},{6,5},{7,6},{8,11},{9,8},{10,9... | collective-permute-start | bytes 1228808 | tf_op jit(solution)/shard_map/ppermute | solution.py:165
  105.1 2.0 fusion.23
  107.8 1.5 convolution_add_fusion.3
  109.2 7.0 %collective-permute-done.8 = bf16[64,5,640]{2,0,1:T(8,128)(2,1)S(1)} collective-permute-done((bf16[64,5,640]{2,0,1:T(8,128)(2,1)S(1)}, bf16[64,5,640]{2,0,1:T(8,128)(2,1)S(1)}, u32[]{:S(2)}, u32[]{:S(2)}) %collective-permute-start.8) | collective-permute-done | bytes 409632 | tf_op jit(solution)/shard_map/ppermute | solution.py:165
  116.8 2.4 %collective-permute-done.6 = bf16[64,5,640]{2,0,1:T(8,128)(2,1)S(1)} collective-permute-done((bf16[64,5,640]{2,0,1:T(8,128)(2,1)S(1)}, bf16[64,5,640]{2,0,1:T(8,128)(2,1)S(1)}, u32[]{:S(2)}, u32[]{:S(2)}) %collective-permute-start.6) | collective-permute-done | bytes 409632 | tf_op jit(solution)/shard_map/ppermute | solution.py:165
  119.7 6.1 %collective-permute-done.7 = bf16[64,5,640]{2,0,1:T(8,128)(2,1)S(1)} collective-permute-done((bf16[64,5,640]{2,0,1:T(8,128)(2,1)S(1)}, bf16[64,5,640]{2,0,1:T(8,128)(2,1)S(1)}, u32[]{:S(2)}, u32[]{:S(2)}) %collective-permute-start.7) | collective-permute-done | bytes 409632 | tf_op jit(solution)/shard_map/ppermute | solution.py:165
  128.7 2.9 %collective-permute-start.11 = (bf16[64,5,640]{2,0,1:T(8,128)(2,1)S(1)}, bf16[64,5,640]{2,0,1:T(8,128)(2,1)S(1)}, u32[]{:S(2)}, u32[]{:S(2)}) collective-permute-start(bf16[64,5,640]{2,0,1:T(8,128)(2,1)S(1)} %get-tuple-element.14), channel_id=1, source_target_pairs={{0,3},{1,0},{2,1},{3,2},{4,7},{5,4},{6,5},{7,6},{8,11},{9,8},{10,9... | collective-permute-start | bytes 1228808 | tf_op jit(solution)/shard_map/ppermute | solution.py:165
  133.1 2.4 %fusion.16 = f32[64,4,2,384]{3,0,2,1:T(8,128)} fusion(f32[64,4,2,384]{3,0,2,1:T(8,128)S(1)} %fusion.24, f32[64,4,2,384]{3,0,2,1:T(8,128)S(1)} %convolution_add_fusion.3, bf16[1,640,2,384]{3,2,1,0:T(2,128)(2,1)S(1)} %get-tuple-element.9, bf16[64,4,640]{2,0,1:T(8,128)(2,1)} %collective-permute-done.13), kind=kOutput, calls=%fused_computation.16 | convolution fusion | flops 252051456 | bytes 3670016 | tf_op jit(solution)/shard_map/snc,cgf->sngf/dot_general | solution.py:253
  135.5 4.2 %collective-permute-done.10 = bf16[64,5,640]{2,0,1:T(8,128)(2,1)S(1)} collective-permute-done((bf16[64,5,640]{2,0,1:T(8,128)(2,1)S(1)}, bf16[64,5,640]{2,0,1:T(8,128)(2,1)S(1)}, u32[]{:S(2)}, u32[]{:S(2)}) %collective-permute-start.10) | collective-permute-done | bytes 409632 | tf_op jit(solution)/shard_map/ppermute | solution.py:165
  139.7 7.7 %collective-permute-done.11 = bf16[64,5,640]{2,0,1:T(8,128)(2,1)S(1)} collective-permute-done((bf16[64,5,640]{2,0,1:T(8,128)(2,1)S(1)}, bf16[64,5,640]{2,0,1:T(8,128)(2,1)S(1)}, u32[]{:S(2)}, u32[]{:S(2)}) %collective-permute-start.11) | collective-permute-done | bytes 409632 | tf_op jit(solution)/shard_map/ppermute | solution.py:165
  147.4 3.0 %collective-permute-done.9 = bf16[64,5,640]{2,0,1:T(8,128)(2,1)S(1)} collective-permute-done((bf16[64,5,640]{2,0,1:T(8,128)(2,1)S(1)}, bf16[64,5,640]{2,0,1:T(8,128)(2,1)S(1)}, u32[]{:S(2)}, u32[]{:S(2)}) %collective-permute-start.9) | collective-permute-done | bytes 409632 | tf_op jit(solution)/shard_map/ppermute | solution.py:165
  151.7 11.2 %all-to-all-start.1 = ((bf16[64,5,640]{2,1,0:T(8,128)(2,1)}), bf16[64,5,640]{2,1,0:T(8,128)(2,1)S(1)}, u32[]{:S(2)}, u32[]{:S(2)}) async-start(bf16[64,5,640]{2,1,0:T(8,128)(2,1)} %copy.109), calls=%async_computation.1 | async-start | bytes 1310720 | tf_op jit(solution)/shard_map/all_to_all | solution.py:263
  162.9 2.0 fusion.12
  165.2 3.3 %collective-permute-start.16 = (bf16[64,4,640]{2,0,1:T(8,128)(2,1)S(1)}, bf16[64,4,640]{2,0,1:T(8,128)(2,1)S(1)}, u32[]{:S(2)}, u32[]{:S(2)}) collective-permute-start(bf16[64,4,640]{2,0,1:T(8,128)(2,1)S(1)} %get-tuple-element.18), channel_id=1, source_target_pairs={{0,2},{1,3},{2,0},{3,1},{4,6},{5,7},{6,4},{7,5},{8,10},{9,11},{10,... | collective-permute-start | bytes 983048 | tf_op jit(solution)/shard_map/ppermute | solution.py:165
  168.5 6.7 %collective-permute-done.15 = bf16[64,4,640]{2,0,1:T(8,128)(2,1)S(1)} collective-permute-done((bf16[64,4,640]{2,0,1:T(8,128)(2,1)S(1)}, bf16[64,4,640]{2,0,1:T(8,128)(2,1)S(1)}, u32[]{:S(2)}, u32[]{:S(2)}) %collective-permute-start.15) | collective-permute-done | bytes 327712 | tf_op jit(solution)/shard_map/ppermute | solution.py:165
  175.2 7.7 %collective-permute-done.16 = bf16[64,4,640]{2,0,1:T(8,128)(2,1)S(1)} collective-permute-done((bf16[64,4,640]{2,0,1:T(8,128)(2,1)S(1)}, bf16[64,4,640]{2,0,1:T(8,128)(2,1)S(1)}, u32[]{:S(2)}, u32[]{:S(2)}) %collective-permute-start.16) | collective-permute-done | bytes 327712 | tf_op jit(solution)/shard_map/ppermute | solution.py:165
  184.0 11.2 %all-to-all-start.3 = ((bf16[64,4,640]{2,1,0:T(4,128)(2,1)}), bf16[64,4,640]{2,1,0:T(4,128)(2,1)S(1)}, u32[]{:S(2)}, u32[]{:S(2)}) async-start(bf16[64,4,640]{2,1,0:T(4,128)(2,1)} %copy.117), calls=%async_computation.3 | async-start | bytes 655360 | tf_op jit(solution)/shard_map/all_to_all | solution.py:263
  196.1 12.4 %all-to-all-done.3 = bf16[64,4,640]{2,1,0:T(4,128)(2,1)S(1)} async-done(((bf16[64,4,640]{2,1,0:T(4,128)(2,1)}), bf16[64,4,640]{2,1,0:T(4,128)(2,1)S(1)}, u32[]{:S(2)}, u32[]{:S(2)}) %all-to-all-start.3) | async-done | bytes 327712 | tf_op jit(solution)/shard_map/all_to_all | solution.py:263
  (81 shorter events, 31.8 us)
Async XLA Ops:
  11.1 12.2 %copy-start.1 = (bf16[640,2560]{1,0:T(8,128)(2,1)S(1)}, bf16[640,2560]{1,0:T(8,128)(2,1)}, u32[]{:S(2)}) copy-start(bf16[640,2560]{1,0:T(8,128)(2,1)} %param.18) | copy-start | bytes 9830404
  23.4 8.2 %copy-start.6 = (s32[64,6]{0,1:T(8,128)S(1)}, s32[64,6]{0,1:T(8,128)}, u32[]{:S(2)}) copy-start(s32[64,6]{0,1:T(8,128)} %param.20) | copy-start | bytes 4612
  25.0 0.8 copy-start.3
  25.8 6.4 %collective-permute-start = (f32[64,640]{1,0:T(8,128)S(1)}, f32[64,640]{1,0:T(8,128)S(1)}, u32[]{:S(2)}, u32[]{:S(2)}) collective-permute-start(f32[64,640]{1,0:T(8,128)S(1)} %get-tuple-element.19), channel_id=1, source_target_pairs={{0,1},{1,2},{2,3},{3,0},{4,5},{5,6},{6,7},{7,4},{8,9},{9,10},{10,1... | collective-permute-start | bytes 491528 | tf_op jit(solution)/shard_map/ppermute | solution.py:165
  27.9 9.6 %collective-permute-start.1 = (f32[64,640]{1,0:T(8,128)S(1)}, f32[64,640]{1,0:T(8,128)S(1)}, u32[]{:S(2)}, u32[]{:S(2)}) collective-permute-start(f32[64,640]{1,0:T(8,128)S(1)} %get-tuple-element.21), channel_id=1, source_target_pairs={{0,2},{1,3},{2,0},{3,1},{4,6},{5,7},{6,4},{7,5},{8,10},{9,11},{10,... | collective-permute-start | bytes 491528 | tf_op jit(solution)/shard_map/ppermute | solution.py:165
  30.4 7.2 %collective-permute-start.2 = (f32[64,640]{1,0:T(8,128)S(1)}, f32[64,640]{1,0:T(8,128)S(1)}, u32[]{:S(2)}, u32[]{:S(2)}) collective-permute-start(f32[64,640]{1,0:T(8,128)S(1)} %get-tuple-element.20), channel_id=1, source_target_pairs={{0,3},{1,0},{2,1},{3,2},{4,7},{5,4},{6,5},{7,6},{8,11},{9,8},{10,9... | collective-permute-start | bytes 491528 | tf_op jit(solution)/shard_map/ppermute | solution.py:165
  38.7 5.2 %collective-permute-start.3 = (f32[64,1]{0,1:T(1,128)S(1)}, f32[64,1]{0,1:T(1,128)S(1)}, u32[]{:S(2)}, u32[]{:S(2)}) collective-permute-start(f32[64,1]{0,1:T(1,128)S(1)} %bitcast.144), channel_id=1, source_target_pairs={{0,1},{1,2},{2,3},{3,0},{4,5},{5,6},{6,7},{7,4},{8,9},{9,10},{10,1... | collective-permute-start | bytes 776 | tf_op jit(solution)/shard_map/ppermute | solution.py:165
  39.7 4.2 %collective-permute-start.4 = (f32[64,1]{0,1:T(1,128)S(1)}, f32[64,1]{0,1:T(1,128)S(1)}, u32[]{:S(2)}, u32[]{:S(2)}) collective-permute-start(f32[64,1]{0,1:T(1,128)S(1)} %bitcast.145), channel_id=1, source_target_pairs={{0,2},{1,3},{2,0},{3,1},{4,6},{5,7},{6,4},{7,5},{8,10},{9,11},{10,... | collective-permute-start | bytes 776 | tf_op jit(solution)/shard_map/ppermute | solution.py:165
  41.6 2.4 %collective-permute-start.5 = (f32[64,1]{0,1:T(1,128)S(1)}, f32[64,1]{0,1:T(1,128)S(1)}, u32[]{:S(2)}, u32[]{:S(2)}) collective-permute-start(f32[64,1]{0,1:T(1,128)S(1)} %bitcast.146), channel_id=1, source_target_pairs={{0,3},{1,0},{2,1},{3,2},{4,7},{5,4},{6,5},{7,6},{8,11},{9,8},{10,9... | collective-permute-start | bytes 776 | tf_op jit(solution)/shard_map/ppermute | solution.py:165
  45.7 29.1 %all-to-all-start.2 = ((bf16[64,4,640]{2,1,0:T(4,128)(2,1)}), bf16[64,4,640]{2,1,0:T(4,128)(2,1)S(1)}, u32[]{:S(2)}, u32[]{:S(2)}) async-start(bf16[64,4,640]{2,1,0:T(4,128)(2,1)} %slice.50), calls=%async_computation.2 | async-start | bytes 655360 | tf_op jit(solution)/shard_map/all_to_all | solution.py:244
  74.8 26.3 %all-to-all-start = ((bf16[64,5,640]{2,1,0:T(8,128)(2,1)}), bf16[64,5,640]{2,1,0:T(8,128)(2,1)}, u32[]{:S(2)}, u32[]{:S(2)}) async-start(bf16[64,5,640]{2,1,0:T(8,128)(2,1)} %slice.46), calls=%async_computation | async-start | bytes 1310720 | tf_op jit(solution)/shard_map/all_to_all | solution.py:244
  89.8 4.2 %copy-start = (bf16[1,640,2,384]{3,2,1,0:T(2,128)(2,1)}, bf16[1,640,2,384]{3,2,1,0:T(2,128)(2,1)S(1)}, u32[]{:S(2)}) copy-start(bf16[1,640,2,384]{3,2,1,0:T(2,128)(2,1)S(1)} %get-tuple-element.11) | copy-start | bytes 2949124
  90.6 16.4 %collective-permute-start.12 = (bf16[64,4,640]{2,0,1:T(8,128)(2,1)}, bf16[64,4,640]{2,0,1:T(8,128)(2,1)}, u32[]{:S(2)}, u32[]{:S(2)}) collective-permute-start(bf16[64,4,640]{2,0,1:T(8,128)(2,1)} %copy.113), channel_id=1, source_target_pairs={{0,1},{1,2},{2,3},{3,0},{4,5},{5,6},{6,7},{7,4},{8,9},{9,10},{10,1... | collective-permute-start | bytes 983048 | tf_op jit(solution)/shard_map/ppermute | solution.py:165
  90.6 41.0 %collective-permute-start.14 = (bf16[64,4,640]{2,0,1:T(8,128)(2,1)}, bf16[64,4,640]{2,0,1:T(8,128)(2,1)}, u32[]{:S(2)}, u32[]{:S(2)}) collective-permute-start(bf16[64,4,640]{2,0,1:T(8,128)(2,1)} %copy.113), channel_id=1, source_target_pairs={{0,3},{1,0},{2,1},{3,2},{4,7},{5,4},{6,5},{7,6},{8,11},{9,8},{10,9... | collective-permute-start | bytes 983048 | tf_op jit(solution)/shard_map/ppermute | solution.py:165
  93.3 39.8 %collective-permute-start.13 = (bf16[64,4,640]{2,0,1:T(8,128)(2,1)}, bf16[64,4,640]{2,0,1:T(8,128)(2,1)}, u32[]{:S(2)}, u32[]{:S(2)}) collective-permute-start(bf16[64,4,640]{2,0,1:T(8,128)(2,1)} %copy.113), channel_id=1, source_target_pairs={{0,2},{1,3},{2,0},{3,1},{4,6},{5,7},{6,4},{7,5},{8,10},{9,11},{10,... | collective-permute-start | bytes 983048 | tf_op jit(solution)/shard_map/ppermute | solution.py:165
  101.1 6.7 %copy-start.2 = (f32[64,4,2,384]{3,0,2,1:T(8,128)S(1)}, f32[64,4,2,384]{3,0,2,1:T(8,128)}, u32[]{:S(2)}) copy-start(f32[64,4,2,384]{3,0,2,1:T(8,128)} %fusion.22) | copy-start | bytes 2359300
  102.3 16.8 %collective-permute-start.6 = (bf16[64,5,640]{2,0,1:T(8,128)(2,1)S(1)}, bf16[64,5,640]{2,0,1:T(8,128)(2,1)S(1)}, u32[]{:S(2)}, u32[]{:S(2)}) collective-permute-start(bf16[64,5,640]{2,0,1:T(8,128)(2,1)S(1)} %copy.102), channel_id=1, source_target_pairs={{0,1},{1,2},{2,3},{3,0},{4,5},{5,6},{6,7},{7,4},{8,9},{9,10},{10,1... | collective-permute-start | bytes 1228808 | tf_op jit(solution)/shard_map/ppermute | solution.py:165
  102.4 13.8 %collective-permute-start.8 = (bf16[64,5,640]{2,0,1:T(8,128)(2,1)S(1)}, bf16[64,5,640]{2,0,1:T(8,128)(2,1)S(1)}, u32[]{:S(2)}, u32[]{:S(2)}) collective-permute-start(bf16[64,5,640]{2,0,1:T(8,128)(2,1)S(1)} %copy.102), channel_id=1, source_target_pairs={{0,3},{1,0},{2,1},{3,2},{4,7},{5,4},{6,5},{7,6},{8,11},{9,8},{10,9... | collective-permute-start | bytes 1228808 | tf_op jit(solution)/shard_map/ppermute | solution.py:165
  107.1 18.8 %collective-permute-start.7 = (bf16[64,5,640]{2,0,1:T(8,128)(2,1)S(1)}, bf16[64,5,640]{2,0,1:T(8,128)(2,1)S(1)}, u32[]{:S(2)}, u32[]{:S(2)}) collective-permute-start(bf16[64,5,640]{2,0,1:T(8,128)(2,1)S(1)} %copy.102), channel_id=1, source_target_pairs={{0,2},{1,3},{2,0},{3,1},{4,6},{5,7},{6,4},{7,5},{8,10},{9,11},{10,... | collective-permute-start | bytes 1228808 | tf_op jit(solution)/shard_map/ppermute | solution.py:165
  125.9 1.5 copy-start.4
  128.6 11.1 %collective-permute-start.10 = (bf16[64,5,640]{2,0,1:T(8,128)(2,1)S(1)}, bf16[64,5,640]{2,0,1:T(8,128)(2,1)S(1)}, u32[]{:S(2)}, u32[]{:S(2)}) collective-permute-start(bf16[64,5,640]{2,0,1:T(8,128)(2,1)S(1)} %get-tuple-element.15), channel_id=1, source_target_pairs={{0,2},{1,3},{2,0},{3,1},{4,6},{5,7},{6,4},{7,5},{8,10},{9,11},{10,... | collective-permute-start | bytes 1228808 | tf_op jit(solution)/shard_map/ppermute | solution.py:165
  128.7 18.7 %collective-permute-start.11 = (bf16[64,5,640]{2,0,1:T(8,128)(2,1)S(1)}, bf16[64,5,640]{2,0,1:T(8,128)(2,1)S(1)}, u32[]{:S(2)}, u32[]{:S(2)}) collective-permute-start(bf16[64,5,640]{2,0,1:T(8,128)(2,1)S(1)} %get-tuple-element.14), channel_id=1, source_target_pairs={{0,3},{1,0},{2,1},{3,2},{4,7},{5,4},{6,5},{7,6},{8,11},{9,8},{10,9... | collective-permute-start | bytes 1228808 | tf_op jit(solution)/shard_map/ppermute | solution.py:165
  131.7 18.7 %collective-permute-start.9 = (bf16[64,5,640]{2,0,1:T(8,128)(2,1)S(1)}, bf16[64,5,640]{2,0,1:T(8,128)(2,1)S(1)}, u32[]{:S(2)}, u32[]{:S(2)}) collective-permute-start(bf16[64,5,640]{2,0,1:T(8,128)(2,1)S(1)} %get-tuple-element.13), channel_id=1, source_target_pairs={{0,1},{1,2},{2,3},{3,0},{4,5},{5,6},{6,7},{7,4},{8,9},{9,10},{10,1... | collective-permute-start | bytes 1228808 | tf_op jit(solution)/shard_map/ppermute | solution.py:165
  135.5 27.4 %copy-start.5 = (bf16[384,4,640]{2,1,0:T(4,128)(2,1)S(1)}, bf16[384,4,640]{2,1,0:T(4,128)(2,1)}, u32[]{:S(2)}) copy-start(bf16[384,4,640]{2,1,0:T(4,128)(2,1)} %reshape_squeeze.3) | copy-start | bytes 5898244
  151.7 32.4 %all-to-all-start.1 = ((bf16[64,5,640]{2,1,0:T(8,128)(2,1)}), bf16[64,5,640]{2,1,0:T(8,128)(2,1)S(1)}, u32[]{:S(2)}, u32[]{:S(2)}) async-start(bf16[64,5,640]{2,1,0:T(8,128)(2,1)} %copy.109), calls=%async_computation.1 | async-start | bytes 1310720 | tf_op jit(solution)/shard_map/all_to_all | solution.py:263
  165.1 30.2 %copy-start.7 = (f32[64,6]{0,1:T(8,128)S(1)}, f32[64,6]{0,1:T(8,128)}, u32[]{:S(2)}) copy-start(f32[64,6]{0,1:T(8,128)} %param.21) | copy-start | bytes 4612
  165.1 10.1 %collective-permute-start.15 = (bf16[64,4,640]{2,0,1:T(8,128)(2,1)S(1)}, bf16[64,4,640]{2,0,1:T(8,128)(2,1)S(1)}, u32[]{:S(2)}, u32[]{:S(2)}) collective-permute-start(bf16[64,4,640]{2,0,1:T(8,128)(2,1)S(1)} %get-tuple-element.16), channel_id=1, source_target_pairs={{0,1},{1,2},{2,3},{3,0},{4,5},{5,6},{6,7},{7,4},{8,9},{9,10},{10,1... | collective-permute-start | bytes 983048 | tf_op jit(solution)/shard_map/ppermute | solution.py:165
  165.2 17.7 %collective-permute-start.16 = (bf16[64,4,640]{2,0,1:T(8,128)(2,1)S(1)}, bf16[64,4,640]{2,0,1:T(8,128)(2,1)S(1)}, u32[]{:S(2)}, u32[]{:S(2)}) collective-permute-start(bf16[64,4,640]{2,0,1:T(8,128)(2,1)S(1)} %get-tuple-element.18), channel_id=1, source_target_pairs={{0,2},{1,3},{2,0},{3,1},{4,6},{5,7},{6,4},{7,5},{8,10},{9,11},{10,... | collective-permute-start | bytes 983048 | tf_op jit(solution)/shard_map/ppermute | solution.py:165
  168.5 14.4 %collective-permute-start.17 = (bf16[64,4,640]{2,0,1:T(8,128)(2,1)S(1)}, bf16[64,4,640]{2,0,1:T(8,128)(2,1)S(1)}, u32[]{:S(2)}, u32[]{:S(2)}) collective-permute-start(bf16[64,4,640]{2,0,1:T(8,128)(2,1)S(1)} %get-tuple-element.17), channel_id=1, source_target_pairs={{0,3},{1,0},{2,1},{3,2},{4,7},{5,4},{6,5},{7,6},{8,11},{9,8},{10,9... | collective-permute-start | bytes 983048 | tf_op jit(solution)/shard_map/ppermute | solution.py:165
  184.0 24.5 %all-to-all-start.3 = ((bf16[64,4,640]{2,1,0:T(4,128)(2,1)}), bf16[64,4,640]{2,1,0:T(4,128)(2,1)S(1)}, u32[]{:S(2)}, u32[]{:S(2)}) async-start(bf16[64,4,640]{2,1,0:T(4,128)(2,1)} %copy.117), calls=%async_computation.3 | async-start | bytes 655360 | tf_op jit(solution)/shard_map/all_to_all | solution.py:263

commit v5 on v4

--- a/solution.py
+++ b/solution.py
@@ -12,27 +12,40 @@
 
 
 def attention_kernel(
-    first_ref, long_ref, info_ref, q_ref, new_k_ref, new_v_ref, len_ref, kv_hbm, o_ref,
+    table_ref, len_ref, base_ref, q_ref, new_k_ref, new_v_ref, kv_hbm, o_ref,
     short_k, short_v, long_k, long_v, sem,
 ):
     rows = q_ref.shape[0]
     head_dim = new_k_ref.shape[1]
     groups = q_ref.shape[1] // head_dim
-    table_width = long_ref.shape[0]
+    table_width = table_ref.shape[1]
+    pool_pages = kv_hbm.shape[1]
     page_size = kv_hbm.shape[2]
     chunk = 16
     scale_of_score = 1.0 / math.sqrt(head_dim)
+    base = base_ref[0]
+
+    def local_page(r, j):
+        return jnp.minimum(jnp.maximum(table_ref[r, j] - base, 0), pool_pages - 1)
+
+    def longest(r, carry):
+        best_row, best_len = carry
+        length = len_ref[r]
+        better = length > best_len
+        return jnp.where(better, r, best_row), jnp.where(better, length, best_len)
+
+    long_row, long_len = lax.fori_loop(0, rows, longest, (jnp.int32(0), len_ref[0]))
 
     def short_copy(r, which, buf):
         return pltpu.make_async_copy(
-            kv_hbm.at[which, first_ref[r], pl.ds(0, SHORT), :],
+            kv_hbm.at[which, local_page(r, 0), pl.ds(0, SHORT), :],
             buf.at[pl.ds(r * SHORT, SHORT), :],
             sem.at[which, r],
         )
 
     def long_copy(j, which, buf):
         return pltpu.make_async_copy(
-            kv_hbm.at[which, long_ref[j]],
+            kv_hbm.at[which, local_page(long_row, j)],
             buf.at[pl.ds(j * page_size, page_size), :],
             sem.at[2 + which, j],
         )
@@ -82,7 +95,9 @@
         k0 = pl.multiple_of(c * width, width)
         keys = short_k[pl.ds(k0, width), :]
         values = short_v[pl.ds(k0, width), :]
-        lengths = jnp.minimum(len_ref[pl.ds(r0, chunk), :], SHORT)
+        lengths = jnp.zeros((chunk, 1), jnp.int32)
+        for i in range(chunk):
+            lengths = jnp.where(row[:, :1] == i, jnp.minimum(len_ref[r0 + i], SHORT), lengths)
         valid = (col >= row * SHORT) & (col < row * SHORT + lengths)
         new_k = new_k_ref[pl.ds(r0, chunk), :]
         new_v = new_v_ref[pl.ds(r0, chunk), :]
@@ -97,8 +112,6 @@
         long_copy(j, 0, long_k).wait()
         long_copy(j, 1, long_v).wait()
 
-    long_row = info_ref[0]
-    long_len = info_ref[1]
     long_col = lax.broadcasted_iota(jnp.int32, (chunk, table_width * page_size), 1)
     long_valid = long_col < long_len
     own_row = lax.broadcasted_iota(jnp.int32, (chunk, 1), 0)
@@ -124,18 +137,14 @@
     page_size = key_value_pages.shape[2]
     head_dim = HEAD_SIZE
     table_width = page_table.shape[1]
-    local_pages = jnp.clip(page_table - lax.axis_index("dp") * pool_pages, 0, pool_pages - 1)
-    long_row = jnp.argmax(cache_len).astype(jnp.int32)
-    info = jnp.stack([long_row, jnp.max(cache_len)]).astype(jnp.int32)
-    first = local_pages[:, 0]
-    long_pages = local_pages[long_row]
+    base = jnp.full((1,), lax.axis_index("dp") * pool_pages, jnp.int32)
     smem = pl.BlockSpec(memory_space=pltpu.SMEM)
     vmem = pl.BlockSpec(memory_space=pltpu.VMEM)
     rows = row_count * SHORT + table_width * page_size
     return pl.pallas_call(
         attention_kernel,
         out_shape=jax.ShapeDtypeStruct(query.shape, jnp.bfloat16),
-        in_specs=[smem, smem, smem, vmem, vmem, vmem, vmem, pl.BlockSpec(memory_space=pl.ANY)],
+        in_specs=[smem, smem, smem, vmem, vmem, vmem, pl.BlockSpec(memory_space=pl.ANY)],
         out_specs=vmem,
         scratch_shapes=[
             pltpu.VMEM((row_count * SHORT, head_dim), key_value_pages.dtype),
@@ -149,16 +158,7 @@
             transcendentals=16 * query.shape[1] // head_dim * rows,
             bytes_accessed=2 * 2 * head_dim * rows,
         ),
-    )(
-        first,
-        long_pages,
-        info,
-        query,
-        new_kv[0],
-        new_kv[1],
-        cache_len[:, None],
-        key_value_pages,
-    )
+    )(page_table, cache_len, base, query, new_kv[0], new_kv[1], key_value_pages)
 
 
 def ring_shift(x, shift, axis_name, size):

time: 210 us -> 203 us (0.967)
  other arithmetic: 7.16 us -> 1.88 us
    another operation x2 -> x0, other arithmetic: 3.27 us -> none  [the longest x1 1.94 us: local_attention(): info = jnp.stack([long_row, jnp.max(cache_len)]).astype(jnp.int32)]
where the time goes in v5:
time: 203 us; the launch traced here: 202 us
  waiting for transfers between devices  80 us (39%)
  starting transfers between devices  68 us (33%)
  local copies, waits for them, and re-layouts  21.2 us (10%)
  matrix products  16.9 us (8%)
  Pallas kernels  13.3 us (7%)
    ppermute x18, waiting for transfers between devices, ring_shift(): lax.ppermute(x, axis_name, [(i, (i + shift) % size) for i in range(size)])  49.9 us
    ppermute x18, starting transfers between devices, ring_shift(): lax.ppermute(x, axis_name, [(i, (i + shift) % size) for i in range(size)])  24.4 us
    all_to_all x2, starting transfers between devices, per_device(): lax.all_to_all(expert_sum, 'dp', split_axis=0, concat_axis=0, tiled=True)  22.1 us
    all_to_all x2, starting transfers between devices, per_device(): lax.all_to_all(outgoing[:, lo:hi], 'dp', split_axis=0, concat_axis=0, til...  21.5 us
    all_to_all x2, waiting for transfers between devices, per_device(): lax.all_to_all(outgoing[:, lo:hi], 'dp', split_axis=0, concat_axis=0, til...  17.7 us
    pallas_call x1, Pallas kernels, local_attention(): pl.pallas_call(attention_kernel, out_shape=jax.ShapeDtypeStruct(query.sha...  13.3 us
    all_to_all x2, waiting for transfers between devices, per_device(): lax.all_to_all(expert_sum, 'dp', split_axis=0, concat_axis=0, tiled=True)  12.4 us
    dot_general x8, matrix products, per_device(): jnp.einsum('snc,cgf->sngf', piece, weight, preferred_element_type=jnp.flo...  10.3 us
  transfers between devices with their start and end apart: 22, of which 13 were waited for; matrix products, arithmetic and copies ran while one was open for 14% of the time, Pallas kernels for 0%

profile of v5, /device:TPU:1, one launch (start us, length us, event | category | flops | bytes accessed | tf_op | source)
XLA Modules:
  0.0 201.8 jit_solution(7524258335170135461)
XLA Ops:
  1.3 1.4 copy.94.table_ref
  2.8 13.3 %shard_map.118 = bf16[64,640]{1,0:T(8,128)(2,1)} custom-call(s32[64,32]{1,0:T(8,128)} %copy.94.table_ref, s32[64]{0:T(128)} %len_ref.1, s32[1]{0:T(128)} %bitcast.base_ref, bf16[64,640]{1,0:T(8,128)(2,1)} %q_ref.1, bf16[64,128]{1,0:T(8,128)(2,1)} %get-tuple-element.21.new_k_ref, bf16[64,128]{1,0:T(8,128)(2,1)} %get-tuple-element.20.new_v_ref, ...), custom_call_target="tpu_custom_call" | custom-call | flops 335544320 | bytes 4194304 | tf_op jit(solution)/shard_map/pallas_call | solution.py:144
  16.0 1.6 fusion
  18.5 2.1 %collective-permute-start = (f32[64,640]{1,0:T(8,128)S(1)}, f32[64,640]{1,0:T(8,128)S(1)}, u32[]{:S(2)}, u32[]{:S(2)}) collective-permute-start(f32[64,640]{1,0:T(8,128)S(1)} %get-tuple-element.17), channel_id=1, source_target_pairs={{0,1},{1,2},{2,3},{3,0},{4,5},{5,6},{6,7},{7,4},{8,9},{9,10},{10,1... | collective-permute-start | bytes 491528 | tf_op jit(solution)/shard_map/ppermute | solution.py:165
  20.6 2.5 %collective-permute-start.1 = (f32[64,640]{1,0:T(8,128)S(1)}, f32[64,640]{1,0:T(8,128)S(1)}, u32[]{:S(2)}, u32[]{:S(2)}) collective-permute-start(f32[64,640]{1,0:T(8,128)S(1)} %get-tuple-element.19), channel_id=1, source_target_pairs={{0,2},{1,3},{2,0},{3,1},{4,6},{5,7},{6,4},{7,5},{8,10},{9,11},{10,... | collective-permute-start | bytes 491528 | tf_op jit(solution)/shard_map/ppermute | solution.py:165
  24.9 5.3 %collective-permute-done.1 = f32[64,640]{1,0:T(8,128)S(1)} collective-permute-done((f32[64,640]{1,0:T(8,128)S(1)}, f32[64,640]{1,0:T(8,128)S(1)}, u32[]{:S(2)}, u32[]{:S(2)}) %collective-permute-start.1) | collective-permute-done | bytes 163872 | tf_op jit(solution)/shard_map/ppermute | solution.py:165
  32.4 1.9 collective-permute-start.4
  38.4 15.2 %all-to-all-start.2 = ((bf16[64,4,640]{2,1,0:T(4,128)(2,1)}), bf16[64,4,640]{2,1,0:T(4,128)(2,1)S(1)}, u32[]{:S(2)}, u32[]{:S(2)}) async-start(bf16[64,4,640]{2,1,0:T(4,128)(2,1)} %slice.45), calls=%async_computation.2 | async-start | bytes 655360 | tf_op jit(solution)/shard_map/all_to_all | solution.py:244
  54.5 12.4 %all-to-all-done.2 = bf16[64,4,640]{2,1,0:T(4,128)(2,1)S(1)} async-done(((bf16[64,4,640]{2,1,0:T(4,128)(2,1)}), bf16[64,4,640]{2,1,0:T(4,128)(2,1)S(1)}, u32[]{:S(2)}, u32[]{:S(2)}) %all-to-all-start.2) | async-done | bytes 327712 | tf_op jit(solution)/shard_map/all_to_all | solution.py:244
  66.8 6.3 %all-to-all-start = ((bf16[64,5,640]{2,1,0:T(8,128)(2,1)}), bf16[64,5,640]{2,1,0:T(8,128)(2,1)}, u32[]{:S(2)}, u32[]{:S(2)}) async-start(bf16[64,5,640]{2,1,0:T(8,128)(2,1)} %slice.41), calls=%async_computation | async-start | bytes 1310720 | tf_op jit(solution)/shard_map/all_to_all | solution.py:244
  73.2 4.5 %reshape_squeeze.3 = bf16[384,4,640]{2,1,0:T(4,128)(2,1)} reshape(bf16[1,384,2560]{2,1,0:T(8,128)(2,1)} %param.23) | data formatting | bytes 3932160 | tf_op jit(solution)/shard_map/reshape;squeeze | solution.py:238
  77.7 4.2 %constant_dynamic-slice_fusion.1 = (bf16[1,640,2,384]{3,2,1,0:T(2,128)(2,1)S(1)}, bf16[1,640,2,384]{3,2,1,0:T(2,128)(2,1)S(1)}, bf16[1,640,2,384]{3,2,1,0:T(2,128)(2,1)S(1)}, bf16[1,640,2,384]{3,2,1,0:T(2,128)(2,1)S(1)}) fusion(bf16[4,640,2,384]{3,2,1,0:T(2,128)(2,1)} %bitcast.137, s32[]{:T(128)S(6)} %select_n.113, s32[]{:T(128)S(6)} %select_n.111, ...), kind=kLoop, calls=%fused_computation.87 | loop fusion | bytes 7864336 | tf_op jit(solution)/shard_map/jit(dynamic_index_in_dim)/dynamic_slice | solution.py:250
  82.9 2.6 %collective-permute-start.14 = (bf16[64,4,640]{2,0,1:T(8,128)(2,1)}, bf16[64,4,640]{2,0,1:T(8,128)(2,1)}, u32[]{:S(2)}, u32[]{:S(2)}) collective-permute-start(bf16[64,4,640]{2,0,1:T(8,128)(2,1)} %copy.113), channel_id=1, source_target_pairs={{0,3},{1,0},{2,1},{3,2},{4,7},{5,4},{6,5},{7,6},{8,11},{9,8},{10,9... | collective-permute-start | bytes 983048 | tf_op jit(solution)/shard_map/ppermute | solution.py:165
  87.8 5.3 %all-to-all-done = bf16[64,5,640]{2,1,0:T(8,128)(2,1)} async-done(((bf16[64,5,640]{2,1,0:T(8,128)(2,1)}), bf16[64,5,640]{2,1,0:T(8,128)(2,1)}, u32[]{:S(2)}, u32[]{:S(2)}) %all-to-all-start) | async-done | bytes 409632 | tf_op jit(solution)/shard_map/all_to_all | solution.py:244
  94.6 2.6 %collective-permute-start.8 = (bf16[64,5,640]{2,0,1:T(8,128)(2,1)S(1)}, bf16[64,5,640]{2,0,1:T(8,128)(2,1)S(1)}, u32[]{:S(2)}, u32[]{:S(2)}) collective-permute-start(bf16[64,5,640]{2,0,1:T(8,128)(2,1)S(1)} %copy.102), channel_id=1, source_target_pairs={{0,3},{1,0},{2,1},{3,2},{4,7},{5,4},{6,5},{7,6},{8,11},{9,8},{10,9... | collective-permute-start | bytes 1228808 | tf_op jit(solution)/shard_map/ppermute | solution.py:165
  97.1 2.0 fusion.23
  100.2 1.5 convolution_add_fusion.3
  101.7 7.1 %collective-permute-done.8 = bf16[64,5,640]{2,0,1:T(8,128)(2,1)S(1)} collective-permute-done((bf16[64,5,640]{2,0,1:T(8,128)(2,1)S(1)}, bf16[64,5,640]{2,0,1:T(8,128)(2,1)S(1)}, u32[]{:S(2)}, u32[]{:S(2)}) %collective-permute-start.8) | collective-permute-done | bytes 409632 | tf_op jit(solution)/shard_map/ppermute | solution.py:165
  109.3 2.3 %collective-permute-done.6 = bf16[64,5,640]{2,0,1:T(8,128)(2,1)S(1)} collective-permute-done((bf16[64,5,640]{2,0,1:T(8,128)(2,1)S(1)}, bf16[64,5,640]{2,0,1:T(8,128)(2,1)S(1)}, u32[]{:S(2)}, u32[]{:S(2)}) %collective-permute-start.6) | collective-permute-done | bytes 409632 | tf_op jit(solution)/shard_map/ppermute | solution.py:165
  112.2 6.1 %collective-permute-done.7 = bf16[64,5,640]{2,0,1:T(8,128)(2,1)S(1)} collective-permute-done((bf16[64,5,640]{2,0,1:T(8,128)(2,1)S(1)}, bf16[64,5,640]{2,0,1:T(8,128)(2,1)S(1)}, u32[]{:S(2)}, u32[]{:S(2)}) %collective-permute-start.7) | collective-permute-done | bytes 409632 | tf_op jit(solution)/shard_map/ppermute | solution.py:165
  121.2 3.0 %collective-permute-start.11 = (bf16[64,5,640]{2,0,1:T(8,128)(2,1)S(1)}, bf16[64,5,640]{2,0,1:T(8,128)(2,1)S(1)}, u32[]{:S(2)}, u32[]{:S(2)}) collective-permute-start(bf16[64,5,640]{2,0,1:T(8,128)(2,1)S(1)} %get-tuple-element.12), channel_id=1, source_target_pairs={{0,3},{1,0},{2,1},{3,2},{4,7},{5,4},{6,5},{7,6},{8,11},{9,8},{10,9... | collective-permute-start | bytes 1228808 | tf_op jit(solution)/shard_map/ppermute | solution.py:165
  124.5 1.4 fusion.24
  126.0 2.4 %fusion.16 = f32[64,4,2,384]{3,0,2,1:T(8,128)} fusion(f32[64,4,2,384]{3,0,2,1:T(8,128)S(1)} %fusion.24, f32[64,4,2,384]{3,0,2,1:T(8,128)S(1)} %convolution_add_fusion.3, bf16[1,640,2,384]{3,2,1,0:T(2,128)(2,1)S(1)} %get-tuple-element.7, bf16[64,4,640]{2,0,1:T(8,128)(2,1)} %collective-permute-done.13), kind=kOutput, calls=%fused_computation.16 | convolution fusion | flops 252051456 | bytes 3670016 | tf_op jit(solution)/shard_map/snc,cgf->sngf/dot_general | solution.py:253
  128.3 3.9 %collective-permute-done.10 = bf16[64,5,640]{2,0,1:T(8,128)(2,1)S(1)} collective-permute-done((bf16[64,5,640]{2,0,1:T(8,128)(2,1)S(1)}, bf16[64,5,640]{2,0,1:T(8,128)(2,1)S(1)}, u32[]{:S(2)}, u32[]{:S(2)}) %collective-permute-start.10) | collective-permute-done | bytes 409632 | tf_op jit(solution)/shard_map/ppermute | solution.py:165
  132.2 9.9 %collective-permute-done.11 = bf16[64,5,640]{2,0,1:T(8,128)(2,1)S(1)} collective-permute-done((bf16[64,5,640]{2,0,1:T(8,128)(2,1)S(1)}, bf16[64,5,640]{2,0,1:T(8,128)(2,1)S(1)}, u32[]{:S(2)}, u32[]{:S(2)}) %collective-permute-start.11) | collective-permute-done | bytes 409632 | tf_op jit(solution)/shard_map/ppermute | solution.py:165
  144.2 10.9 %all-to-all-start.1 = ((bf16[64,5,640]{2,1,0:T(8,128)(2,1)}), bf16[64,5,640]{2,1,0:T(8,128)(2,1)S(1)}, u32[]{:S(2)}, u32[]{:S(2)}) async-start(bf16[64,5,640]{2,1,0:T(8,128)(2,1)} %copy.109), calls=%async_computation.1 | async-start | bytes 1310720 | tf_op jit(solution)/shard_map/all_to_all | solution.py:263
  155.1 2.0 fusion.12
  157.7 3.1 %collective-permute-start.16 = (bf16[64,4,640]{2,0,1:T(8,128)(2,1)S(1)}, bf16[64,4,640]{2,0,1:T(8,128)(2,1)S(1)}, u32[]{:S(2)}, u32[]{:S(2)}) collective-permute-start(bf16[64,4,640]{2,0,1:T(8,128)(2,1)S(1)} %get-tuple-element.16), channel_id=1, source_target_pairs={{0,2},{1,3},{2,0},{3,1},{4,6},{5,7},{6,4},{7,5},{8,10},{9,11},{10,... | collective-permute-start | bytes 983048 | tf_op jit(solution)/shard_map/ppermute | solution.py:165
  160.8 6.5 %collective-permute-done.15 = bf16[64,4,640]{2,0,1:T(8,128)(2,1)S(1)} collective-permute-done((bf16[64,4,640]{2,0,1:T(8,128)(2,1)S(1)}, bf16[64,4,640]{2,0,1:T(8,128)(2,1)S(1)}, u32[]{:S(2)}, u32[]{:S(2)}) %collective-permute-start.15) | collective-permute-done | bytes 327712 | tf_op jit(solution)/shard_map/ppermute | solution.py:165
  167.3 7.9 %collective-permute-done.16 = bf16[64,4,640]{2,0,1:T(8,128)(2,1)S(1)} collective-permute-done((bf16[64,4,640]{2,0,1:T(8,128)(2,1)S(1)}, bf16[64,4,640]{2,0,1:T(8,128)(2,1)S(1)}, u32[]{:S(2)}, u32[]{:S(2)}) %collective-permute-start.16) | collective-permute-done | bytes 327712 | tf_op jit(solution)/shard_map/ppermute | solution.py:165
  176.4 11.2 %all-to-all-start.3 = ((bf16[64,4,640]{2,1,0:T(4,128)(2,1)}), bf16[64,4,640]{2,1,0:T(4,128)(2,1)S(1)}, u32[]{:S(2)}, u32[]{:S(2)}) async-start(bf16[64,4,640]{2,1,0:T(4,128)(2,1)} %copy.117), calls=%async_computation.3 | async-start | bytes 655360 | tf_op jit(solution)/shard_map/all_to_all | solution.py:263
  188.5 12.4 %all-to-all-done.3 = bf16[64,4,640]{2,1,0:T(4,128)(2,1)S(1)} async-done(((bf16[64,4,640]{2,1,0:T(4,128)(2,1)}), bf16[64,4,640]{2,1,0:T(4,128)(2,1)S(1)}, u32[]{:S(2)}, u32[]{:S(2)}) %all-to-all-start.3) | async-done | bytes 327712 | tf_op jit(solution)/shard_map/all_to_all | solution.py:263
  (75 shorter events, 26.9 us)
Async XLA Ops:
  2.7 13.3 %copy-start.1 = (bf16[640,2560]{1,0:T(8,128)(2,1)S(1)}, bf16[640,2560]{1,0:T(8,128)(2,1)}, u32[]{:S(2)}) copy-start(bf16[640,2560]{1,0:T(8,128)(2,1)} %param.18) | copy-start | bytes 9830404
  16.0 8.2 %copy-start.6 = (s32[64,6]{0,1:T(8,128)S(1)}, s32[64,6]{0,1:T(8,128)}, u32[]{:S(2)}) copy-start(s32[64,6]{0,1:T(8,128)} %param.20) | copy-start | bytes 4612
  17.6 0.8 copy-start.3
  18.5 6.4 %collective-permute-start = (f32[64,640]{1,0:T(8,128)S(1)}, f32[64,640]{1,0:T(8,128)S(1)}, u32[]{:S(2)}, u32[]{:S(2)}) collective-permute-start(f32[64,640]{1,0:T(8,128)S(1)} %get-tuple-element.17), channel_id=1, source_target_pairs={{0,1},{1,2},{2,3},{3,0},{4,5},{5,6},{6,7},{7,4},{8,9},{9,10},{10,1... | collective-permute-start | bytes 491528 | tf_op jit(solution)/shard_map/ppermute | solution.py:165
  20.6 9.6 %collective-permute-start.1 = (f32[64,640]{1,0:T(8,128)S(1)}, f32[64,640]{1,0:T(8,128)S(1)}, u32[]{:S(2)}, u32[]{:S(2)}) collective-permute-start(f32[64,640]{1,0:T(8,128)S(1)} %get-tuple-element.19), channel_id=1, source_target_pairs={{0,2},{1,3},{2,0},{3,1},{4,6},{5,7},{6,4},{7,5},{8,10},{9,11},{10,... | collective-permute-start | bytes 491528 | tf_op jit(solution)/shard_map/ppermute | solution.py:165
  23.1 7.2 %collective-permute-start.2 = (f32[64,640]{1,0:T(8,128)S(1)}, f32[64,640]{1,0:T(8,128)S(1)}, u32[]{:S(2)}, u32[]{:S(2)}) collective-permute-start(f32[64,640]{1,0:T(8,128)S(1)} %get-tuple-element.18), channel_id=1, source_target_pairs={{0,3},{1,0},{2,1},{3,2},{4,7},{5,4},{6,5},{7,6},{8,11},{9,8},{10,9... | collective-permute-start | bytes 491528 | tf_op jit(solution)/shard_map/ppermute | solution.py:165
  31.4 5.2 %collective-permute-start.3 = (f32[64,1]{0,1:T(1,128)S(1)}, f32[64,1]{0,1:T(1,128)S(1)}, u32[]{:S(2)}, u32[]{:S(2)}) collective-permute-start(f32[64,1]{0,1:T(1,128)S(1)} %bitcast.140), channel_id=1, source_target_pairs={{0,1},{1,2},{2,3},{3,0},{4,5},{5,6},{6,7},{7,4},{8,9},{9,10},{10,1... | collective-permute-start | bytes 776 | tf_op jit(solution)/shard_map/ppermute | solution.py:165
  32.4 4.2 %collective-permute-start.4 = (f32[64,1]{0,1:T(1,128)S(1)}, f32[64,1]{0,1:T(1,128)S(1)}, u32[]{:S(2)}, u32[]{:S(2)}) collective-permute-start(f32[64,1]{0,1:T(1,128)S(1)} %bitcast.141), channel_id=1, source_target_pairs={{0,2},{1,3},{2,0},{3,1},{4,6},{5,7},{6,4},{7,5},{8,10},{9,11},{10,... | collective-permute-start | bytes 776 | tf_op jit(solution)/shard_map/ppermute | solution.py:165
  34.3 2.4 %collective-permute-start.5 = (f32[64,1]{0,1:T(1,128)S(1)}, f32[64,1]{0,1:T(1,128)S(1)}, u32[]{:S(2)}, u32[]{:S(2)}) collective-permute-start(f32[64,1]{0,1:T(1,128)S(1)} %bitcast.142), channel_id=1, source_target_pairs={{0,3},{1,0},{2,1},{3,2},{4,7},{5,4},{6,5},{7,6},{8,11},{9,8},{10,9... | collective-permute-start | bytes 776 | tf_op jit(solution)/shard_map/ppermute | solution.py:165
  38.4 28.4 %all-to-all-start.2 = ((bf16[64,4,640]{2,1,0:T(4,128)(2,1)}), bf16[64,4,640]{2,1,0:T(4,128)(2,1)S(1)}, u32[]{:S(2)}, u32[]{:S(2)}) async-start(bf16[64,4,640]{2,1,0:T(4,128)(2,1)} %slice.45), calls=%async_computation.2 | async-start | bytes 655360 | tf_op jit(solution)/shard_map/all_to_all | solution.py:244
  66.8 26.3 %all-to-all-start = ((bf16[64,5,640]{2,1,0:T(8,128)(2,1)}), bf16[64,5,640]{2,1,0:T(8,128)(2,1)}, u32[]{:S(2)}, u32[]{:S(2)}) async-start(bf16[64,5,640]{2,1,0:T(8,128)(2,1)} %slice.41), calls=%async_computation | async-start | bytes 1310720 | tf_op jit(solution)/shard_map/all_to_all | solution.py:244
  81.9 4.5 %copy-start = (bf16[1,640,2,384]{3,2,1,0:T(2,128)(2,1)}, bf16[1,640,2,384]{3,2,1,0:T(2,128)(2,1)S(1)}, u32[]{:S(2)}) copy-start(bf16[1,640,2,384]{3,2,1,0:T(2,128)(2,1)S(1)} %get-tuple-element.9) | copy-start | bytes 2949124
  82.8 16.4 %collective-permute-start.12 = (bf16[64,4,640]{2,0,1:T(8,128)(2,1)}, bf16[64,4,640]{2,0,1:T(8,128)(2,1)}, u32[]{:S(2)}, u32[]{:S(2)}) collective-permute-start(bf16[64,4,640]{2,0,1:T(8,128)(2,1)} %copy.113), channel_id=1, source_target_pairs={{0,1},{1,2},{2,3},{3,0},{4,5},{5,6},{6,7},{7,4},{8,9},{9,10},{10,1... | collective-permute-start | bytes 983048 | tf_op jit(solution)/shard_map/ppermute | solution.py:165
  82.9 41.6 %collective-permute-start.14 = (bf16[64,4,640]{2,0,1:T(8,128)(2,1)}, bf16[64,4,640]{2,0,1:T(8,128)(2,1)}, u32[]{:S(2)}, u32[]{:S(2)}) collective-permute-start(bf16[64,4,640]{2,0,1:T(8,128)(2,1)} %copy.113), channel_id=1, source_target_pairs={{0,3},{1,0},{2,1},{3,2},{4,7},{5,4},{6,5},{7,6},{8,11},{9,8},{10,9... | collective-permute-start | bytes 983048 | tf_op jit(solution)/shard_map/ppermute | solution.py:165
  85.4 40.5 %collective-permute-start.13 = (bf16[64,4,640]{2,0,1:T(8,128)(2,1)}, bf16[64,4,640]{2,0,1:T(8,128)(2,1)}, u32[]{:S(2)}, u32[]{:S(2)}) collective-permute-start(bf16[64,4,640]{2,0,1:T(8,128)(2,1)} %copy.113), channel_id=1, source_target_pairs={{0,2},{1,3},{2,0},{3,1},{4,6},{5,7},{6,4},{7,5},{8,10},{9,11},{10,... | collective-permute-start | bytes 983048 | tf_op jit(solution)/shard_map/ppermute | solution.py:165
  93.2 7.0 %copy-start.2 = (f32[64,4,2,384]{3,0,2,1:T(8,128)S(1)}, f32[64,4,2,384]{3,0,2,1:T(8,128)}, u32[]{:S(2)}) copy-start(f32[64,4,2,384]{3,0,2,1:T(8,128)} %fusion.22) | copy-start | bytes 2359300
  94.4 17.3 %collective-permute-start.6 = (bf16[64,5,640]{2,0,1:T(8,128)(2,1)S(1)}, bf16[64,5,640]{2,0,1:T(8,128)(2,1)S(1)}, u32[]{:S(2)}, u32[]{:S(2)}) collective-permute-start(bf16[64,5,640]{2,0,1:T(8,128)(2,1)S(1)} %copy.102), channel_id=1, source_target_pairs={{0,1},{1,2},{2,3},{3,0},{4,5},{5,6},{6,7},{7,4},{8,9},{9,10},{10,1... | collective-permute-start | bytes 1228808 | tf_op jit(solution)/shard_map/ppermute | solution.py:165
  94.6 14.2 %collective-permute-start.8 = (bf16[64,5,640]{2,0,1:T(8,128)(2,1)S(1)}, bf16[64,5,640]{2,0,1:T(8,128)(2,1)S(1)}, u32[]{:S(2)}, u32[]{:S(2)}) collective-permute-start(bf16[64,5,640]{2,0,1:T(8,128)(2,1)S(1)} %copy.102), channel_id=1, source_target_pairs={{0,3},{1,0},{2,1},{3,2},{4,7},{5,4},{6,5},{7,6},{8,11},{9,8},{10,9... | collective-permute-start | bytes 1228808 | tf_op jit(solution)/shard_map/ppermute | solution.py:165
  99.1 19.3 %collective-permute-start.7 = (bf16[64,5,640]{2,0,1:T(8,128)(2,1)S(1)}, bf16[64,5,640]{2,0,1:T(8,128)(2,1)S(1)}, u32[]{:S(2)}, u32[]{:S(2)}) collective-permute-start(bf16[64,5,640]{2,0,1:T(8,128)(2,1)S(1)} %copy.102), channel_id=1, source_target_pairs={{0,2},{1,3},{2,0},{3,1},{4,6},{5,7},{6,4},{7,5},{8,10},{9,11},{10,... | collective-permute-start | bytes 1228808 | tf_op jit(solution)/shard_map/ppermute | solution.py:165
  118.4 1.5 copy-start.4
  121.1 11.1 %collective-permute-start.10 = (bf16[64,5,640]{2,0,1:T(8,128)(2,1)S(1)}, bf16[64,5,640]{2,0,1:T(8,128)(2,1)S(1)}, u32[]{:S(2)}, u32[]{:S(2)}) collective-permute-start(bf16[64,5,640]{2,0,1:T(8,128)(2,1)S(1)} %get-tuple-element.13), channel_id=1, source_target_pairs={{0,2},{1,3},{2,0},{3,1},{4,6},{5,7},{6,4},{7,5},{8,10},{9,11},{10,... | collective-permute-start | bytes 1228808 | tf_op jit(solution)/shard_map/ppermute | solution.py:165
  121.2 20.9 %collective-permute-start.11 = (bf16[64,5,640]{2,0,1:T(8,128)(2,1)S(1)}, bf16[64,5,640]{2,0,1:T(8,128)(2,1)S(1)}, u32[]{:S(2)}, u32[]{:S(2)}) collective-permute-start(bf16[64,5,640]{2,0,1:T(8,128)(2,1)S(1)} %get-tuple-element.12), channel_id=1, source_target_pairs={{0,3},{1,0},{2,1},{3,2},{4,7},{5,4},{6,5},{7,6},{8,11},{9,8},{10,9... | collective-permute-start | bytes 1228808 | tf_op jit(solution)/shard_map/ppermute | solution.py:165
  124.2 18.7 %collective-permute-start.9 = (bf16[64,5,640]{2,0,1:T(8,128)(2,1)S(1)}, bf16[64,5,640]{2,0,1:T(8,128)(2,1)S(1)}, u32[]{:S(2)}, u32[]{:S(2)}) collective-permute-start(bf16[64,5,640]{2,0,1:T(8,128)(2,1)S(1)} %get-tuple-element.11), channel_id=1, source_target_pairs={{0,1},{1,2},{2,3},{3,0},{4,5},{5,6},{6,7},{7,4},{8,9},{9,10},{10,1... | collective-permute-start | bytes 1228808 | tf_op jit(solution)/shard_map/ppermute | solution.py:165
  128.3 26.7 %copy-start.5 = (bf16[384,4,640]{2,1,0:T(4,128)(2,1)S(1)}, bf16[384,4,640]{2,1,0:T(4,128)(2,1)}, u32[]{:S(2)}) copy-start(bf16[384,4,640]{2,1,0:T(4,128)(2,1)} %reshape_squeeze.3) | copy-start | bytes 5898244
  144.2 32.2 %all-to-all-start.1 = ((bf16[64,5,640]{2,1,0:T(8,128)(2,1)}), bf16[64,5,640]{2,1,0:T(8,128)(2,1)S(1)}, u32[]{:S(2)}, u32[]{:S(2)}) async-start(bf16[64,5,640]{2,1,0:T(8,128)(2,1)} %copy.109), calls=%async_computation.1 | async-start | bytes 1310720 | tf_op jit(solution)/shard_map/all_to_all | solution.py:263
  157.2 30.4 %copy-start.7 = (f32[64,6]{0,1:T(8,128)S(1)}, f32[64,6]{0,1:T(8,128)}, u32[]{:S(2)}) copy-start(f32[64,6]{0,1:T(8,128)} %param.21) | copy-start | bytes 4612
  157.2 10.1 %collective-permute-start.15 = (bf16[64,4,640]{2,0,1:T(8,128)(2,1)S(1)}, bf16[64,4,640]{2,0,1:T(8,128)(2,1)S(1)}, u32[]{:S(2)}, u32[]{:S(2)}) collective-permute-start(bf16[64,4,640]{2,0,1:T(8,128)(2,1)S(1)} %get-tuple-element.14), channel_id=1, source_target_pairs={{0,1},{1,2},{2,3},{3,0},{4,5},{5,6},{6,7},{7,4},{8,9},{9,10},{10,1... | collective-permute-start | bytes 983048 | tf_op jit(solution)/shard_map/ppermute | solution.py:165
  157.7 17.5 %collective-permute-start.16 = (bf16[64,4,640]{2,0,1:T(8,128)(2,1)S(1)}, bf16[64,4,640]{2,0,1:T(8,128)(2,1)S(1)}, u32[]{:S(2)}, u32[]{:S(2)}) collective-permute-start(bf16[64,4,640]{2,0,1:T(8,128)(2,1)S(1)} %get-tuple-element.16), channel_id=1, source_target_pairs={{0,2},{1,3},{2,0},{3,1},{4,6},{5,7},{6,4},{7,5},{8,10},{9,11},{10,... | collective-permute-start | bytes 983048 | tf_op jit(solution)/shard_map/ppermute | solution.py:165
  160.8 14.4 %collective-permute-start.17 = (bf16[64,4,640]{2,0,1:T(8,128)(2,1)S(1)}, bf16[64,4,640]{2,0,1:T(8,128)(2,1)S(1)}, u32[]{:S(2)}, u32[]{:S(2)}) collective-permute-start(bf16[64,4,640]{2,0,1:T(8,128)(2,1)S(1)} %get-tuple-element.15), channel_id=1, source_target_pairs={{0,3},{1,0},{2,1},{3,2},{4,7},{5,4},{6,5},{7,6},{8,11},{9,8},{10,9... | collective-permute-start | bytes 983048 | tf_op jit(solution)/shard_map/ppermute | solution.py:165
  176.4 24.5 %all-to-all-start.3 = ((bf16[64,4,640]{2,1,0:T(4,128)(2,1)}), bf16[64,4,640]{2,1,0:T(4,128)(2,1)S(1)}, u32[]{:S(2)}, u32[]{:S(2)}) async-start(bf16[64,4,640]{2,1,0:T(4,128)(2,1)} %copy.117), calls=%async_computation.3 | async-start | bytes 655360 | tf_op jit(solution)/shard_map/all_to_all | solution.py:263
